TPU v7x, 256 devices: a whole 4x4x8 slice. The times are simulated.
256 devices in a mesh: chan: 64 (over x, y, z_hi, core), beam: 4 (over z_lo).
Axes of the slice: x: 4, y: 4, z: 8 (z_hi: 2, z_lo: 4; z = z_hi * 4 + z_lo), core: 2. Of those that a mesh axis runs over, the one named last changes fastest.
Arguments:
- images: float32 [256, 36, 128, 128], P('chan', 'beam')
- beam_weight: float32 [36, 128, 128], P('beam'), may hold values from 0.2 to 1
- offsets: int32 [36, 2], P('beam'), may hold values from 0 to 384, as said below
- rejected_indicator: int32 [256, 192, 512], P('chan', None, 'beam'), may hold values 0 or 1
- regression_indicator: int32 [256], replicated, may hold values 0 or 1
Outputs:
- cleaned_cube: float32 [256, 192, 512], P(None, 'chan', 'beam')
Inputs may be any that keep to these rules, and one draw needn't show every extreme that they name: `offsets`: beam b = 6 r + q sits near row r * 64 // 5 and column q * 384 // 5, within 16; every sky pixel is covered by some beam; the first and last row and column of beams lie at the field's edges.
All inputs are finite; a program needn't handle non-finite values. No bound on the sum of `rejected_indicator` on one device may be relied on, other than what follows from the above.
Results may differ from a plain program's by a relative error of at most 0.00023.
Values sent between devices are 32-bit elements; how exact they have to be, the bound alone decides.
No kernel may reach another device: no remote copies, remote signals or barrier semaphores. Data moves between devices by JAX's collectives and lax.ppermute only.
A program may use at most 128 MiB of HBM per device.

v0:
```python
import jax
import jax.numpy as jnp
from jax import lax
from jax.sharding import PartitionSpec as P

MOS_ROWS = 192
MOS_COLS = 512


def legendre(count):
    position = (2.0 * jnp.arange(count).astype(jnp.float32) + 1.0) / count - 1.0
    square = position * position
    return jnp.stack(
        [
            jnp.ones_like(position),
            position,
            0.5 * (3.0 * square - 1.0),
            0.5 * (5.0 * square * position - 3.0 * position),
        ],
        axis=1,
    )


def solve_cubic(normal_matrix, right_side):
    factor = {}
    for outer in range(4):
        for inner in range(outer + 1):
            value = normal_matrix[outer * 4 + inner]
            for other in range(inner):
                value = value - factor[outer, other] * factor[inner, other]
            if outer == inner:
                factor[outer, outer] = jnp.sqrt(value)
            else:
                factor[outer, inner] = value / factor[inner, inner]
    forward = []
    for outer in range(4):
        value = right_side[outer]
        for other in range(outer):
            value = value - factor[outer, other] * forward[other]
        forward.append(value / factor[outer, outer])
    backward = [None] * 4
    for outer in range(3, -1, -1):
        value = forward[outer]
        for other in range(outer + 1, 4):
            value = value - factor[other, outer] * backward[other]
        backward[outer] = value / factor[outer, outer]
    return jnp.stack(backward, axis=0)


def clean_pair(pair):
    sky_tile, weight_tile = pair
    channels, rows, columns = sky_tile.shape
    celestial_image = sky_tile.reshape(channels, rows * columns)
    importance_factor = weight_tile.reshape(channels, rows * columns)
    table = legendre(channels)
    products = jnp.stack(
        [table[:, outer] * table[:, inner] for outer in range(4) for inner in range(4)], axis=0
    )
    normal_matrix = jnp.dot(
        products,
        importance_factor,
        precision=lax.Precision.HIGHEST,
        preferred_element_type=jnp.float32,
    )
    right_side = jnp.dot(
        table.T,
        importance_factor * celestial_image,
        precision=lax.Precision.HIGHEST,
        preferred_element_type=jnp.float32,
    )
    coefficients = solve_cubic(normal_matrix, right_side)
    continuum = jnp.dot(
        table, coefficients, precision=lax.Precision.HIGHEST, preferred_element_type=jnp.float32
    )
    residual = celestial_image - continuum
    padded = jnp.pad(residual, ((1, 1), (0, 0)))
    smoothed = 0.25 * padded[:-2] + 0.5 * residual + 0.25 * padded[2:]
    return smoothed.reshape(channels, rows, columns)


def local(images, beam_weight, offsets, rejected_indicator, regression_indicator):
    ch_dev = images.shape[0]
    beam_dev = images.shape[1]
    side = images.shape[2]
    col_dev = rejected_indicator.shape[2]
    all_channels = regression_indicator.shape[0]
    first_channel = lax.axis_index("chan") * ch_dev
    channel_ids = first_channel + jnp.arange(ch_dev, dtype=jnp.int32)
    exponent = 1.0 + 0.5 * channel_ids.astype(jnp.float32) / (all_channels - 1)
    col_start = lax.axis_index("beam") * col_dev
    empty = jnp.zeros((ch_dev, MOS_ROWS, MOS_COLS), jnp.float32)

    def place(index, state_pair):
        dividend_accumulator, normalizer_accumulated = state_pair
        beam_image = lax.dynamic_index_in_dim(images, index, 1, keepdims=False)
        log_weight = jnp.log(lax.dynamic_index_in_dim(beam_weight, index, 0, keepdims=False))
        response = jnp.exp(exponent[:, None, None] * log_weight[None])
        corner = (jnp.zeros((), jnp.int32), offsets[index, 0], offsets[index, 1])
        extent = (ch_dev, side, side)
        dividend_accumulator = lax.dynamic_update_slice(
            dividend_accumulator,
            lax.dynamic_slice(dividend_accumulator, corner, extent) + response * beam_image,
            corner,
        )
        normalizer_accumulated = lax.dynamic_update_slice(
            normalizer_accumulated,
            lax.dynamic_slice(normalizer_accumulated, corner, extent) + response * response,
            corner,
        )
        return (dividend_accumulator, normalizer_accumulated)

    dividend_accumulator, normalizer_accumulated = lax.fori_loop(0, beam_dev, place, (empty, empty))
    whole_numerator, whole_weight = lax.psum((dividend_accumulator, normalizer_accumulated), "beam")
    dividend_accumulator = lax.dynamic_slice_in_dim(whole_numerator, col_start, col_dev, 2)
    normalizer_accumulated = lax.dynamic_slice_in_dim(whole_weight, col_start, col_dev, 2)
    accepted_entries = 1.0 - rejected_indicator.astype(jnp.float32)
    emission_absent = lax.dynamic_slice_in_dim(regression_indicator, first_channel, ch_dev).astype(
        jnp.float32
    )
    celestial_image = accepted_entries * dividend_accumulator / normalizer_accumulated
    importance_factor = normalizer_accumulated * (
        emission_absent[:, None, None] * accepted_entries + 0.01
    )
    arrived = (
        lax.all_to_all(celestial_image, "chan", split_axis=1, concat_axis=0, tiled=True),
        lax.all_to_all(importance_factor, "chan", split_axis=1, concat_axis=0, tiled=True),
    )
    return clean_pair(arrived)


def solution(mesh):
    in_specs = (
        P("chan", "beam", None, None),
        P("beam", None, None),
        P("beam", None),
        P("chan", None, "beam"),
        P(),
    )
    out_specs = P(None, "chan", "beam")
    return jax.shard_map(local, mesh=mesh, in_specs=in_specs, out_specs=out_specs, check_vma=False)
```

profile of v0, /device:TPU:65, one launch (start us, length us, event | category | flops | bytes accessed | tf_op | source)
XLA Modules:
  0.0 574.9 jit_solution(8023418686840628340)
XLA Ops:
  8.1 367.6 %while.16 = (s32[]{:T(128)}, f32[4,192,512]{2,0,1:T(4,128)S(1)}, f32[4,192,512]{2,0,1:T(4,128)}, s32[9,2]{0,1:T(2,128)S(1)}, f32[9,128,128]{2,1,0:T(8,128)}, /*i...) while((s32[]{:T(128)}, f32[4,192,512]{2,0,1:T(4,128)S(1)}, ...), condition=%wide.region_1.2_spmd.clone, body=%wide.region_0.1_spmd.clone.sunk | while | flops 327704 | bytes 4653321 | solution.py:112
  16.1 4.4 dynamic_update_slice.18
  20.6 5.5 dynamic_update_slice.19
  34.1 21.6 %dynamic_update_slice.18 = f32[4,192,512]{2,0,1:T(4,128)S(1)} dynamic-update-slice(f32[4,192,512]{2,0,1:T(4,128)S(1)} %get-tuple-element.284, f32[4,128,128]{2,0,1:T(4,128)S(1)} %copy.61, s32[]{:T(128)} %constant.76.clone.1..sunk, s32[]{:T(128)S(6)} %select_n.43, s32[]{:T(128)S(6)} %select_n.44) | dynamic-update-slice | bytes 524292 | tf_op jit(solution)/shard_map/while/body/eval_jaxpr/dynamic_update_slice | solution.py:100
  55.8 22.7 %dynamic_update_slice.19 = f32[4,192,512]{2,0,1:T(4,128)} dynamic-update-slice(f32[4,192,512]{2,0,1:T(4,128)} %get-tuple-element.285, f32[4,128,128]{2,0,1:T(4,128)S(1)} %copy.62, s32[]{:T(128)} %constant.76.clone.1..sunk, s32[]{:T(128)S(6)} %select_n.43, s32[]{:T(128)S(6)} %select_n.44) | dynamic-update-slice | bytes 524292 | tf_op jit(solution)/shard_map/while/body/eval_jaxpr/dynamic_update_slice | solution.py:105
  86.5 21.6 %dynamic_update_slice.18 = f32[4,192,512]{2,0,1:T(4,128)S(1)} dynamic-update-slice(f32[4,192,512]{2,0,1:T(4,128)S(1)} %get-tuple-element.284, f32[4,128,128]{2,0,1:T(4,128)S(1)} %copy.61, s32[]{:T(128)} %constant.76.clone.1..sunk, s32[]{:T(128)S(6)} %select_n.43, s32[]{:T(128)S(6)} %select_n.44) | dynamic-update-slice | bytes 524292 | tf_op jit(solution)/shard_map/while/body/eval_jaxpr/dynamic_update_slice | solution.py:100
  108.3 22.7 %dynamic_update_slice.19 = f32[4,192,512]{2,0,1:T(4,128)} dynamic-update-slice(f32[4,192,512]{2,0,1:T(4,128)} %get-tuple-element.285, f32[4,128,128]{2,0,1:T(4,128)S(1)} %copy.62, s32[]{:T(128)} %constant.76.clone.1..sunk, s32[]{:T(128)S(6)} %select_n.43, s32[]{:T(128)S(6)} %select_n.44) | dynamic-update-slice | bytes 524292 | tf_op jit(solution)/shard_map/while/body/eval_jaxpr/dynamic_update_slice | solution.py:105
  139.0 21.6 %dynamic_update_slice.18 = f32[4,192,512]{2,0,1:T(4,128)S(1)} dynamic-update-slice(f32[4,192,512]{2,0,1:T(4,128)S(1)} %get-tuple-element.284, f32[4,128,128]{2,0,1:T(4,128)S(1)} %copy.61, s32[]{:T(128)} %constant.76.clone.1..sunk, s32[]{:T(128)S(6)} %select_n.43, s32[]{:T(128)S(6)} %select_n.44) | dynamic-update-slice | bytes 524292 | tf_op jit(solution)/shard_map/while/body/eval_jaxpr/dynamic_update_slice | solution.py:100
  160.7 22.7 %dynamic_update_slice.19 = f32[4,192,512]{2,0,1:T(4,128)} dynamic-update-slice(f32[4,192,512]{2,0,1:T(4,128)} %get-tuple-element.285, f32[4,128,128]{2,0,1:T(4,128)S(1)} %copy.62, s32[]{:T(128)} %constant.76.clone.1..sunk, s32[]{:T(128)S(6)} %select_n.43, s32[]{:T(128)S(6)} %select_n.44) | dynamic-update-slice | bytes 524292 | tf_op jit(solution)/shard_map/while/body/eval_jaxpr/dynamic_update_slice | solution.py:105
  191.4 21.6 %dynamic_update_slice.18 = f32[4,192,512]{2,0,1:T(4,128)S(1)} dynamic-update-slice(f32[4,192,512]{2,0,1:T(4,128)S(1)} %get-tuple-element.284, f32[4,128,128]{2,0,1:T(4,128)S(1)} %copy.61, s32[]{:T(128)} %constant.76.clone.1..sunk, s32[]{:T(128)S(6)} %select_n.43, s32[]{:T(128)S(6)} %select_n.44) | dynamic-update-slice | bytes 524292 | tf_op jit(solution)/shard_map/while/body/eval_jaxpr/dynamic_update_slice | solution.py:100
  213.1 22.7 %dynamic_update_slice.19 = f32[4,192,512]{2,0,1:T(4,128)} dynamic-update-slice(f32[4,192,512]{2,0,1:T(4,128)} %get-tuple-element.285, f32[4,128,128]{2,0,1:T(4,128)S(1)} %copy.62, s32[]{:T(128)} %constant.76.clone.1..sunk, s32[]{:T(128)S(6)} %select_n.43, s32[]{:T(128)S(6)} %select_n.44) | dynamic-update-slice | bytes 524292 | tf_op jit(solution)/shard_map/while/body/eval_jaxpr/dynamic_update_slice | solution.py:105
  243.7 4.2 dynamic_update_slice.18
  248.1 4.9 dynamic_update_slice.19
  260.9 4.4 dynamic_update_slice.18
  265.5 5.5 dynamic_update_slice.19
  278.9 21.6 %dynamic_update_slice.18 = f32[4,192,512]{2,0,1:T(4,128)S(1)} dynamic-update-slice(f32[4,192,512]{2,0,1:T(4,128)S(1)} %get-tuple-element.284, f32[4,128,128]{2,0,1:T(4,128)S(1)} %copy.61, s32[]{:T(128)} %constant.76.clone.1..sunk, s32[]{:T(128)S(6)} %select_n.43, s32[]{:T(128)S(6)} %select_n.44) | dynamic-update-slice | bytes 524292 | tf_op jit(solution)/shard_map/while/body/eval_jaxpr/dynamic_update_slice | solution.py:100
  300.7 22.7 %dynamic_update_slice.19 = f32[4,192,512]{2,0,1:T(4,128)} dynamic-update-slice(f32[4,192,512]{2,0,1:T(4,128)} %get-tuple-element.285, f32[4,128,128]{2,0,1:T(4,128)S(1)} %copy.62, s32[]{:T(128)} %constant.76.clone.1..sunk, s32[]{:T(128)S(6)} %select_n.43, s32[]{:T(128)S(6)} %select_n.44) | dynamic-update-slice | bytes 524292 | tf_op jit(solution)/shard_map/while/body/eval_jaxpr/dynamic_update_slice | solution.py:105
  331.3 21.6 %dynamic_update_slice.18 = f32[4,192,512]{2,0,1:T(4,128)S(1)} dynamic-update-slice(f32[4,192,512]{2,0,1:T(4,128)S(1)} %get-tuple-element.284, f32[4,128,128]{2,0,1:T(4,128)S(1)} %copy.61, s32[]{:T(128)} %constant.76.clone.1..sunk, s32[]{:T(128)S(6)} %select_n.43, s32[]{:T(128)S(6)} %select_n.44) | dynamic-update-slice | bytes 524292 | tf_op jit(solution)/shard_map/while/body/eval_jaxpr/dynamic_update_slice | solution.py:100
  353.1 22.7 %dynamic_update_slice.19 = f32[4,192,512]{2,0,1:T(4,128)} dynamic-update-slice(f32[4,192,512]{2,0,1:T(4,128)} %get-tuple-element.285, f32[4,128,128]{2,0,1:T(4,128)S(1)} %copy.62, s32[]{:T(128)} %constant.76.clone.1..sunk, s32[]{:T(128)S(6)} %select_n.43, s32[]{:T(128)S(6)} %select_n.44) | dynamic-update-slice | bytes 524292 | tf_op jit(solution)/shard_map/while/body/eval_jaxpr/dynamic_update_slice | solution.py:105
  377.0 133.4 %all-reduce.4.cloned.1.call-done = (f32[4,192,512]{2,0,1:T(4,128)}, f32[4,192,512]{2,0,1:T(4,128)}) async-done(((f32[4,192,512]{2,0,1:T(4,128)}, f32[4,192,512]{2,0,1:T(4,128)}), (f32[4,192,512]{2,0,1:T(4,128)}, f32[4,192,512]{2,0,1:T(4,128)})) %all-reduce.4.cloned.1.call-update) | async-done | bytes 3145744 | tf_op jit(solution)/shard_map/psum | solution.py:113
  510.4 2.3 add_multiply_fusion
  512.7 29.8 %all_to_all.30 = f32[4,192,128]{2,0,1:T(4,128)S(1)} all-to-all(f32[4,192,128]{2,0,1:T(4,128)S(1)} %get-tuple-element.206), channel_id=1, replica_groups=mesh['chan'=64,'beam'=4] {'chan'}, dimensions={1} | all-to-all | bytes 786432 | tf_op jit(solution)/shard_map/all_to_all | solution.py:125
  542.6 4.5 all-to-all-start.1
  547.4 17.8 %all-to-all-done.1 = f32[4,192,128]{2,0,1:T(4,128)S(1)} async-done(((f32[4,192,128]{2,0,1:T(4,128)}), f32[4,192,128]{2,0,1:T(4,128)S(1)}, u32[]{:S(2)}, u32[]{:S(2)}) %all-to-all-start.1) | async-done | bytes 393248 | tf_op jit(solution)/shard_map/all_to_all | solution.py:126
  (97 shorter events, 44.7 us)
Async XLA Ops:
  6.5 503.9 %all-reduce.4.cloned.1.call-start = ((), (), s32[]{:S(2)}) async-start(), calls=%async_computation.2 | async-start | bytes 6291456 | tf_op jit(solution)/shard_map/psum | solution.py:113
  6.5 1.6 copy-start.2
  375.8 1.2 copy-start
  375.8 1.2 copy-start.3
  375.8 134.7 %copy-start.1 = (s32[4,192,128]{2,1,0:T(8,128)S(1)}, s32[4,192,128]{2,1,0:T(8,128)}, u32[]{:S(2)}) copy-start(s32[4,192,128]{2,1,0:T(8,128)} %param.10) | copy-start | bytes 1179652
  542.6 22.7 %all-to-all-start.1 = ((f32[4,192,128]{2,0,1:T(4,128)}), f32[4,192,128]{2,0,1:T(4,128)S(1)}, u32[]{:S(2)}, u32[]{:S(2)}) async-start(f32[4,192,128]{2,0,1:T(4,128)} %get-tuple-element.205), calls=%async_computation.1 | async-start | bytes 786432 | tf_op jit(solution)/shard_map/all_to_all | solution.py:126
Sparse Core Ops, SparseCore 0:
  377.1 133.3 all-reduce.3
where the time goes:
time: 577 us; the launch traced here: 575 us
  local copies, waits for them, and re-layouts  328 us (57%)
  waiting for transfers between devices  151 us (26%)
  loops' own time  34.3 us (6%)
  blocking collectives  29.8 us (5%)
  between operations  13.5 us (2%)
  other arithmetic  12.7 us (2%)
    dynamic_update_slice x18, local copies, waits for them, and re-layouts, place(): lax.dynamic_update_slice(normalizer_accumulated, lax.dynamic_slice(normal...  154 us
    dynamic_update_slice x18, local copies, waits for them, and re-layouts, place(): lax.dynamic_update_slice(dividend_accumulator, lax.dynamic_slice(dividend...  144 us
    psum x1, waiting for transfers between devices, local(): lax.psum((dividend_accumulator, normalizer_accumulated), 'beam')  133 us
    another operation x1, loops' own time, local(): lax.fori_loop(0, beam_dev, place, (empty, empty))  34.3 us
    all_to_all x1, blocking collectives, local(): lax.all_to_all(celestial_image, 'chan', split_axis=1, concat_axis=0, tile...  29.8 us
    all_to_all x1, waiting for transfers between devices, local(): lax.all_to_all(importance_factor, 'chan', split_axis=1, concat_axis=0, ti...  17.8 us
    dynamic_slice x9, local copies, waits for them, and re-layouts, place(): lax.dynamic_slice(normalizer_accumulated, corner, extent)  12.4 us
  transfers between devices with their start and end apart: 2, of which 2 were waited for; matrix products, arithmetic and copies ran while one was open for 0% of the time, Pallas kernels for 0%

commit v1 on v0

--- a/solution.py
+++ b/solution.py
@@ -80,39 +80,33 @@
 
 def local(images, beam_weight, offsets, rejected_indicator, regression_indicator):
     ch_dev = images.shape[0]
-    beam_dev = images.shape[1]
     side = images.shape[2]
-    col_dev = rejected_indicator.shape[2]
     all_channels = regression_indicator.shape[0]
     first_channel = lax.axis_index("chan") * ch_dev
     channel_ids = first_channel + jnp.arange(ch_dev, dtype=jnp.int32)
     exponent = 1.0 + 0.5 * channel_ids.astype(jnp.float32) / (all_channels - 1)
-    col_start = lax.axis_index("beam") * col_dev
-    empty = jnp.zeros((ch_dev, MOS_ROWS, MOS_COLS), jnp.float32)
-
-    def place(index, state_pair):
-        dividend_accumulator, normalizer_accumulated = state_pair
-        beam_image = lax.dynamic_index_in_dim(images, index, 1, keepdims=False)
-        log_weight = jnp.log(lax.dynamic_index_in_dim(beam_weight, index, 0, keepdims=False))
-        response = jnp.exp(exponent[:, None, None] * log_weight[None])
-        corner = (jnp.zeros((), jnp.int32), offsets[index, 0], offsets[index, 1])
-        extent = (ch_dev, side, side)
-        dividend_accumulator = lax.dynamic_update_slice(
-            dividend_accumulator,
-            lax.dynamic_slice(dividend_accumulator, corner, extent) + response * beam_image,
-            corner,
-        )
-        normalizer_accumulated = lax.dynamic_update_slice(
-            normalizer_accumulated,
-            lax.dynamic_slice(normalizer_accumulated, corner, extent) + response * response,
-            corner,
-        )
-        return (dividend_accumulator, normalizer_accumulated)
-
-    dividend_accumulator, normalizer_accumulated = lax.fori_loop(0, beam_dev, place, (empty, empty))
-    whole_numerator, whole_weight = lax.psum((dividend_accumulator, normalizer_accumulated), "beam")
-    dividend_accumulator = lax.dynamic_slice_in_dim(whole_numerator, col_start, col_dev, 2)
-    normalizer_accumulated = lax.dynamic_slice_in_dim(whole_weight, col_start, col_dev, 2)
+    log_weight = jnp.log(beam_weight)
+    response = jnp.exp(exponent[:, None, None, None] * log_weight[None])
+    stacked = jnp.stack([response * images, response * response])
+    row_hit = (
+        lax.broadcasted_iota(jnp.int32, (1, MOS_ROWS, side), 1)
+        == lax.broadcasted_iota(jnp.int32, (1, MOS_ROWS, side), 2) + offsets[:, 0, None, None]
+    ).astype(jnp.float32)
+    col_hit = (
+        lax.broadcasted_iota(jnp.int32, (1, side, MOS_COLS), 2)
+        == lax.broadcasted_iota(jnp.int32, (1, side, MOS_COLS), 1) + offsets[:, 1, None, None]
+    ).astype(jnp.float32)
+    rows_placed = jnp.einsum(
+        "bri,acbij->bacrj", row_hit, stacked, precision=lax.Precision.HIGHEST,
+        preferred_element_type=jnp.float32,
+    )
+    planes = jnp.einsum(
+        "bacrj,bjk->acrk", rows_placed, col_hit, precision=lax.Precision.HIGHEST,
+        preferred_element_type=jnp.float32,
+    )
+    own = lax.psum_scatter(planes, "beam", scatter_dimension=3, tiled=True)
+    dividend_accumulator = own[0]
+    normalizer_accumulated = own[1]
     accepted_entries = 1.0 - rejected_indicator.astype(jnp.float32)
     emission_absent = lax.dynamic_slice_in_dim(regression_indicator, first_channel, ch_dev).astype(
         jnp.float32
@@ -121,11 +115,10 @@
     importance_factor = normalizer_accumulated * (
         emission_absent[:, None, None] * accepted_entries + 0.01
     )
-    arrived = (
-        lax.all_to_all(celestial_image, "chan", split_axis=1, concat_axis=0, tiled=True),
-        lax.all_to_all(importance_factor, "chan", split_axis=1, concat_axis=0, tiled=True),
+    arrived = lax.all_to_all(
+        jnp.stack([celestial_image, importance_factor]), "chan", split_axis=2, concat_axis=1, tiled=True
     )
-    return clean_pair(arrived)
+    return clean_pair((arrived[0], arrived[1]))
 
 
 def solution(mesh):

time: 577 us -> 140 us (0.24)
  local copies, waits for them, and re-layouts: 328 us -> 5.43 us
  waiting for transfers between devices: 151 us -> 94.8 us
  loops' own time: 34.3 us -> 0 us
  blocking collectives: 29.8 us -> 0 us
  matrix products: 1.24 us -> 12.9 us
  other arithmetic: 12.7 us -> 2.52 us
  starting transfers between devices: 4.52 us -> 10.5 us
    dynamic_update_slice x36 -> x0, local copies, waits for them, and re-layouts: 298 us -> none  [the longest x18 154 us: place(): lax.dynamic_update_slice(normalizer_accumulated, lax.dynamic_slice(normal...]
    psum x1 -> x0, waiting for transfers between devices: 133 us -> none  [local(): lax.psum((dividend_accumulator, normalizer_accumulated), 'beam')]
    reduce_scatter x0 -> x1, waiting for transfers between devices: none -> 67.1 us  [local(): own = lax.psum_scatter(planes, 'beam', scatter_dimension=3, tiled=True)]
    another operation x1 -> x0, loops' own time: 34.3 us -> none  [local(): lax.fori_loop(0, beam_dev, place, (empty, empty))]
    all_to_all x1 -> x0, blocking collectives: 29.8 us -> none  [local(): lax.all_to_all(celestial_image, 'chan', split_axis=1, concat_axis=0, tile...]
    dynamic_slice x18 -> x0, local copies, waits for them, and re-layouts: 18 us -> none  [the longest x9 12.4 us: place(): lax.dynamic_slice(normalizer_accumulated, corner, extent)]
    dot_general x0 -> x2, matrix products: none -> 11.6 us  [the longest x1 8.18 us: local(): jnp.einsum('bacrj,bjk->acrk', rows_placed, col_hit, precision=lax.Precisi...]
    all_to_all x1, waiting for transfers between devices: 17.8 us -> 27.7 us  [local(): lax.all_to_all(jnp.stack([celestial_image, importance_factor]), 'chan', s...]
where the time goes in v1:
time: 140 us
  waiting for transfers between devices  94.8 us (68%)
  between operations  13.5 us (10%)
  matrix products  12.9 us (9%)
  starting transfers between devices  10.5 us (8%)
  local copies, waits for them, and re-layouts  5.43 us (4%)
  other arithmetic  2.52 us (2%)
    reduce_scatter x1, waiting for transfers between devices, local(): own = lax.psum_scatter(planes, 'beam', scatter_dimension=3, tiled=True)  67.1 us
    all_to_all x1, waiting for transfers between devices, local(): lax.all_to_all(jnp.stack([celestial_image, importance_factor]), 'chan', s...  27.7 us
    all_to_all x1, starting transfers between devices, local(): lax.all_to_all(jnp.stack([celestial_image, importance_factor]), 'chan', s...  10.5 us
    dot_general x1, matrix products, local(): jnp.einsum('bacrj,bjk->acrk', rows_placed, col_hit, precision=lax.Precisi...  8.18 us
    dot_general x1, matrix products, local(): jnp.einsum('bri,acbij->bacrj', row_hit, stacked, precision=lax.Precision....  3.43 us
  transfers between devices with their start and end apart: 2, of which 2 were waited for; matrix products, arithmetic and copies ran while one was open for 0% of the time, Pallas kernels for 0%

profile of v1, /device:TPU:65, one launch (start us, length us, event | category | flops | bytes accessed | tf_op | source)
XLA Modules:
  0.0 139.6 jit_solution(17191269957032614946)
XLA Ops:
  6.5 1.3 log.3
  7.8 0.4 exponential_multiply_fusion
  8.2 0.1 copy-done
  8.4 0.4 multiply_bitcast_fusion
  8.8 0.3 copy-done.2
  9.1 3.4 %fusion.2 = f32[9,2,4,128,192]{3,4,0,2,1:T(8,128)S(1)} fusion(f32[1,4,9,128,128]{4,3,2,1,0:T(8,128)S(1)} %exponential_multiply_fusion, f32[1,4,9,128,128]{4,3,2,1,0:T(8,128)S(1)} %multiply_bitcast_fusion, s32[9]{0:T(128)S(1)} %get-tuple-element.23), kind=kOutput, calls=%fused_computation.2 | convolution fusion | flops 2719531008 | bytes 11796516 | tf_op jit(solution)/shard_map/bri,acbij->bacrj/dot_general | solution.py:99
  12.5 8.2 %fusion.8 = f32[2,4,192,512]{3,2,1,0:T(8,128)} fusion(f32[9,2,4,128,192]{3,4,0,2,1:T(8,128)S(1)} %fusion.2, s32[9]{0:T(128)S(1)} %get-tuple-element.22), kind=kOutput, calls=%fused_computation.10 | convolution fusion | flops 10872815616 | bytes 10223652 | tf_op jit(solution)/shard_map/bacrj,bjk->acrk/dot_general | solution.py:103
  20.7 0.7 copy-done.3
  21.4 67.1 %reduce-scatter.2.cloned.1.call-done = f32[2,4,192,128]{3,2,1,0:T(8,128)} async-done(((f32[2,4,192,512]{3,2,1,0:T(8,128)}), f32[2,4,192,128]{3,2,1,0:T(8,128)}) %reduce-scatter.2.cloned.1.call-update) | async-done | bytes 786448 | tf_op jit(solution)/shard_map/reduce_scatter | solution.py:107
  88.5 1.2 fusion.23
  89.8 1.4 %copy.14 = f32[2,4,192,128]{3,1,0,2:T(4,128)} copy(f32[2,4,192,128]{3,2,1,0:T(8,128)S(1)} %pad_maximum_fusion) | data formatting | bytes 1572864 | tf_op jit(solution)/shard_map/stack | solution.py:119
  91.2 10.5 %all-to-all-start = ((f32[2,4,192,128]{3,1,0,2:T(4,128)}), f32[2,4,192,128]{3,1,0,2:T(4,128)S(1)}, u32[]{:S(2)}, u32[]{:S(2)}) async-start(f32[2,4,192,128]{3,1,0,2:T(4,128)} %copy.14), calls=%async_computation.1 | async-start | bytes 1572864 | tf_op jit(solution)/shard_map/all_to_all | solution.py:118
  101.9 27.7 %all-to-all-done = f32[2,4,192,128]{3,1,0,2:T(4,128)S(1)} async-done(((f32[2,4,192,128]{3,1,0,2:T(4,128)}), f32[2,4,192,128]{3,1,0,2:T(4,128)S(1)}, u32[]{:S(2)}, u32[]{:S(2)}) %all-to-all-start) | async-done | bytes 786464 | tf_op jit(solution)/shard_map/all_to_all | solution.py:118
  129.6 0.1 copy.15
  129.7 0.1 fusion.60
  129.8 0.1 copy.16
  129.9 0.1 copy.17
  130.1 0.3 fusion.17
  130.4 0.3 fusion.19
  130.7 0.1 fusion.43
  130.9 0.7 convolution_subtract_fusion
  131.5 0.1 multiply_add_fusion
  131.7 0.2 copy.18
  131.8 0.9 copy.19
  (23 shorter events, 0.4 us)
Async XLA Ops:
  6.5 1.8 %copy-start = (f32[4,9,128,128]{3,2,1,0:T(8,128)S(1)}, f32[4,9,128,128]{3,2,1,0:T(8,128)}, u32[]{:S(2)}) copy-start(f32[4,9,128,128]{3,2,1,0:T(8,128)} %param.5) | copy-start | bytes 7077892
  6.5 82.0 %reduce-scatter.2.cloned.1.call-start = ((), (), s32[]{:S(2)}) async-start(), calls=%async_computation.2 | async-start | bytes 3932160 | tf_op jit(solution)/shard_map/reduce_scatter | solution.py:107
  8.4 0.7 copy-start.2
  20.7 0.7 copy-start.3
  20.7 67.8 %copy-start.1 = (s32[4,192,128]{2,1,0:T(8,128)S(1)}, s32[4,192,128]{2,1,0:T(8,128)}, u32[]{:S(2)}) copy-start(s32[4,192,128]{2,1,0:T(8,128)} %param.8) | copy-start | bytes 1179652
  91.2 38.3 %all-to-all-start = ((f32[2,4,192,128]{3,1,0,2:T(4,128)}), f32[2,4,192,128]{3,1,0,2:T(4,128)S(1)}, u32[]{:S(2)}, u32[]{:S(2)}) async-start(f32[2,4,192,128]{3,1,0,2:T(4,128)} %copy.14), calls=%async_computation.1 | async-start | bytes 1572864 | tf_op jit(solution)/shard_map/all_to_all | solution.py:118
Sparse Core Ops, SparseCore 0:
  20.8 67.6 reduce-scatter.1

commit v2 on v1

--- a/solution.py
+++ b/solution.py
@@ -2,6 +2,7 @@
 import jax.numpy as jnp
 from jax import lax
 from jax.sharding import PartitionSpec as P
+
 
 MOS_ROWS = 192
 MOS_COLS = 512
@@ -78,14 +79,11 @@
     return smoothed.reshape(channels, rows, columns)
 
 
-def local(images, beam_weight, offsets, rejected_indicator, regression_indicator):
-    ch_dev = images.shape[0]
+CHUNKS = 2
+
+
+def place_and_reduce(images, log_weight, offsets, exponent, rejected, emission_absent):
     side = images.shape[2]
-    all_channels = regression_indicator.shape[0]
-    first_channel = lax.axis_index("chan") * ch_dev
-    channel_ids = first_channel + jnp.arange(ch_dev, dtype=jnp.int32)
-    exponent = 1.0 + 0.5 * channel_ids.astype(jnp.float32) / (all_channels - 1)
-    log_weight = jnp.log(beam_weight)
     response = jnp.exp(exponent[:, None, None, None] * log_weight[None])
     stacked = jnp.stack([response * images, response * response])
     row_hit = (
@@ -105,20 +103,46 @@
         preferred_element_type=jnp.float32,
     )
     own = lax.psum_scatter(planes, "beam", scatter_dimension=3, tiled=True)
+    own, rejected, emission_absent = lax.optimization_barrier((own, rejected, emission_absent))
     dividend_accumulator = own[0]
     normalizer_accumulated = own[1]
-    accepted_entries = 1.0 - rejected_indicator.astype(jnp.float32)
-    emission_absent = lax.dynamic_slice_in_dim(regression_indicator, first_channel, ch_dev).astype(
-        jnp.float32
-    )
+    accepted_entries = 1.0 - rejected.astype(jnp.float32)
     celestial_image = accepted_entries * dividend_accumulator / normalizer_accumulated
     importance_factor = normalizer_accumulated * (
         emission_absent[:, None, None] * accepted_entries + 0.01
     )
-    arrived = lax.all_to_all(
-        jnp.stack([celestial_image, importance_factor]), "chan", split_axis=2, concat_axis=1, tiled=True
+    return lax.all_to_all(
+        jnp.stack([celestial_image, importance_factor]), "chan", split_axis=2, concat_axis=1,
+        tiled=True,
     )
-    return clean_pair((arrived[0], arrived[1]))
+
+
+def local_body(images, beam_weight, offsets, rejected_indicator, regression_indicator):
+    ch_dev = images.shape[0]
+    all_channels = regression_indicator.shape[0]
+    first_channel = lax.axis_index("chan") * ch_dev
+    channel_ids = first_channel + jnp.arange(ch_dev, dtype=jnp.int32)
+    exponent = 1.0 + 0.5 * channel_ids.astype(jnp.float32) / (all_channels - 1)
+    emission_absent = lax.dynamic_slice_in_dim(regression_indicator, first_channel, ch_dev).astype(
+        jnp.float32
+    )
+    log_weight = jnp.log(beam_weight)
+    per_chunk = ch_dev // CHUNKS
+    parts = []
+    for chunk in range(CHUNKS):
+        window = slice(chunk * per_chunk, (chunk + 1) * per_chunk)
+        parts.append(
+            place_and_reduce(
+                images[window], log_weight, offsets, exponent[window],
+                rejected_indicator[window], emission_absent[window],
+            )
+        )
+    sources = all_channels // ch_dev
+    rows = parts[0].shape[2]
+    gathered = jnp.stack(
+        [part.reshape(2, sources, per_chunk, rows, -1) for part in parts], axis=2
+    ).reshape(2, all_channels, rows, -1)
+    return clean_pair((gathered[0], gathered[1]))
 
 
 def solution(mesh):
@@ -130,4 +154,4 @@
         P(),
     )
     out_specs = P(None, "chan", "beam")
-    return jax.shard_map(local, mesh=mesh, in_specs=in_specs, out_specs=out_specs, check_vma=False)
+    return jax.shard_map(local_body, mesh=mesh, in_specs=in_specs, out_specs=out_specs, check_vma=False)

time: 140 us -> 153 us (1.093)
  starting transfers between devices: 10.5 us -> 20.8 us
  waiting for transfers between devices: 94.8 us -> 91.8 us
  local copies, waits for them, and re-layouts: 5.43 us -> 7.53 us
    all_to_all x1 -> x2, starting transfers between devices: 10.5 us -> 20.7 us  [place_and_reduce(): lax.all_to_all(jnp.stack([celestial_image, importance_factor]), 'chan', s...]
    all_to_all x1 -> x2, waiting for transfers between devices: 27.7 us -> 19.2 us  [place_and_reduce(): lax.all_to_all(jnp.stack([celestial_image, importance_factor]), 'chan', s...]
    reduce_scatter x1 -> x2, waiting for transfers between devices: 67.1 us -> 72.6 us  [place_and_reduce(): own = lax.psum_scatter(planes, 'beam', scatter_dimension=3, tiled=True)]
    dot_general x2 -> x4, matrix products: 11.6 us -> 12.9 us  [the longest x2 9.25 us: place_and_reduce(): jnp.einsum('bacrj,bjk->acrk', rows_placed, col_hit, precision=lax.Precisi...]
  transfers between devices with their start and end apart: 2 -> 4, of which waited for: 2 -> 3; matrix products, arithmetic and copies ran while one was open for 0% -> 7% of each run, Pallas kernels for 0% -> 0%
where the time goes in v2:
time: 153 us; the launch traced here: 152 us
  waiting for transfers between devices  91.8 us (60%)
  starting transfers between devices  20.8 us (14%)
  matrix products  14.1 us (9%)
  between operations  13.6 us (9%)
  local copies, waits for them, and re-layouts  7.53 us (5%)
  other arithmetic  3.91 us (3%)
    reduce_scatter x2, waiting for transfers between devices, place_and_reduce(): own = lax.psum_scatter(planes, 'beam', scatter_dimension=3, tiled=True)  72.6 us
    all_to_all x2, starting transfers between devices, place_and_reduce(): lax.all_to_all(jnp.stack([celestial_image, importance_factor]), 'chan', s...  20.7 us
    all_to_all x2, waiting for transfers between devices, place_and_reduce(): lax.all_to_all(jnp.stack([celestial_image, importance_factor]), 'chan', s...  19.2 us
    dot_general x2, matrix products, place_and_reduce(): jnp.einsum('bacrj,bjk->acrk', rows_placed, col_hit, precision=lax.Precisi...  9.25 us
    dot_general x2, matrix products, place_and_reduce(): jnp.einsum('bri,acbij->bacrj', row_hit, stacked, precision=lax.Precision....  3.65 us
  transfers between devices with their start and end apart: 4, of which 3 were waited for; matrix products, arithmetic and copies ran while one was open for 7% of the time, Pallas kernels for 0%

profile of v2, /device:TPU:65, one launch (start us, length us, event | category | flops | bytes accessed | tf_op | source)
XLA Modules:
  0.0 151.8 jit_solution(9404616707414719658)
XLA Ops:
  6.6 1.1 log.3
  7.8 0.4 exponential_multiply_fusion
  8.2 1.3 copy-done
  9.4 0.4 multiply_bitcast_fusion
  9.8 0.3 copy-done.2
  10.1 1.8 %fusion.4 = f32[9,2,2,128,192]{3,4,0,2,1:T(8,128)S(1)} fusion(f32[1,2,9,128,128]{4,3,2,1,0:T(8,128)S(1)} %get-tuple-element.37, f32[1,2,9,128,128]{4,3,2,1,0:T(8,128)S(1)} %get-tuple-element.31, s32[9]{0:T(128)S(1)} %get-tuple-element.43), kind=kOutput, calls=%fused_computation.4 | convolution fusion | flops 1359986688 | bytes 5898276 | tf_op jit(solution)/shard_map/bri,acbij->bacrj/dot_general | solution.py:97
  12.0 4.6 %fusion.15 = f32[2,2,192,512]{3,2,1,0:T(8,128)} fusion(f32[9,2,2,128,192]{3,4,0,2,1:T(8,128)S(1)} %fusion.4, s32[9]{0:T(128)S(1)} %get-tuple-element.42), kind=kOutput, calls=%fused_computation.14 | convolution fusion | flops 5436997632 | bytes 5111844 | tf_op jit(solution)/shard_map/bacrj,bjk->acrk/dot_general | solution.py:101
  16.6 1.8 %fusion.8 = f32[9,2,2,128,192]{3,4,0,2,1:T(8,128)S(1)} fusion(f32[1,2,9,128,128]{4,3,2,1,0:T(8,128)S(1)} %get-tuple-element.36, f32[1,2,9,128,128]{4,3,2,1,0:T(8,128)S(1)} %get-tuple-element.30, s32[9]{0:T(128)S(1)} %get-tuple-element.43), kind=kOutput, calls=%fused_computation.8 | convolution fusion | flops 1359986688 | bytes 5898276 | tf_op jit(solution)/shard_map/bri,acbij->bacrj/dot_general | solution.py:97
  18.5 4.6 %fusion.20 = f32[2,2,192,512]{3,2,1,0:T(8,128)} fusion(f32[9,2,2,128,192]{3,4,0,2,1:T(8,128)S(1)} %fusion.8, s32[9]{0:T(128)S(1)} %get-tuple-element.42), kind=kOutput, calls=%fused_computation.15 | convolution fusion | flops 5436997632 | bytes 5111844 | tf_op jit(solution)/shard_map/bacrj,bjk->acrk/dot_general | solution.py:101
  23.1 0.7 copy-done.3
  24.2 34.2 %reduce-scatter.3.cloned.1.call-done = f32[2,2,192,128]{3,2,1,0:T(8,128)} async-done(((f32[2,2,192,512]{3,2,1,0:T(8,128)}), f32[2,2,192,128]{3,2,1,0:T(8,128)}) %reduce-scatter.3.cloned.1.call-update) | async-done | bytes 393232 | tf_op jit(solution)/shard_map/reduce_scatter | solution.py:105
  58.4 1.1 fusion.42
  59.5 1.1 copy.15
  60.6 10.5 %all-to-all-start = ((f32[2,2,192,128]{3,1,0,2:T(2,128)}), f32[2,2,192,128]{3,1,0,2:T(2,128)S(1)}, u32[]{:S(2)}, u32[]{:S(2)}) async-start(f32[2,2,192,128]{3,1,0,2:T(2,128)} %copy.15), calls=%async_computation.1 | async-start | bytes 786432 | tf_op jit(solution)/shard_map/all_to_all | solution.py:114
  71.1 38.4 %reduce-scatter.5.cloned.1.call-done = f32[2,2,192,128]{3,2,1,0:T(8,128)} async-done(((f32[2,2,192,512]{3,2,1,0:T(8,128)}), f32[2,2,192,128]{3,2,1,0:T(8,128)}) %reduce-scatter.5.cloned.1.call-update) | async-done | bytes 393232 | tf_op jit(solution)/shard_map/reduce_scatter | solution.py:105
  109.5 1.1 fusion.40
  110.7 1.1 copy.17
  111.7 10.2 %all-to-all-start.1 = ((f32[2,2,192,128]{3,1,0,2:T(2,128)}), f32[2,2,192,128]{3,1,0,2:T(2,128)S(1)}, u32[]{:S(2)}, u32[]{:S(2)}) async-start(f32[2,2,192,128]{3,1,0,2:T(2,128)} %copy.17), calls=%async_computation.3 | async-start | bytes 786432 | tf_op jit(solution)/shard_map/all_to_all | solution.py:114
  122.3 19.2 %all-to-all-done.1 = f32[2,2,192,128]{3,1,0,2:T(2,128)S(1)} async-done(((f32[2,2,192,128]{3,1,0,2:T(2,128)}), f32[2,2,192,128]{3,1,0,2:T(2,128)S(1)}, u32[]{:S(2)}, u32[]{:S(2)}) %all-to-all-start.1) | async-done | bytes 393248 | tf_op jit(solution)/shard_map/all_to_all | solution.py:114
  141.6 0.4 pad_maximum_fusion
  142.3 0.3 fusion.33
  142.6 0.3 fusion.35
  143.1 0.7 convolution_subtract_fusion
  144.0 0.9 copy.22
  (37 shorter events, 1.8 us)
Async XLA Ops:
  6.5 51.8 %reduce-scatter.3.cloned.1.call-start = ((), (), s32[]{:S(2)}) async-start(), calls=%async_computation.4 | async-start | bytes 1966080 | tf_op jit(solution)/shard_map/reduce_scatter | solution.py:105
  7.8 1.7 %copy-start = (f32[4,9,128,128]{3,2,1,0:T(8,128)S(1)}, f32[4,9,128,128]{3,2,1,0:T(8,128)}, u32[]{:S(2)}) copy-start(f32[4,9,128,128]{3,2,1,0:T(8,128)} %param.5) | copy-start | bytes 7077892
  9.4 0.7 copy-start.2
  16.6 92.9 %reduce-scatter.5.cloned.1.call-start = ((), (), s32[]{:S(2)}) async-start(), calls=%async_computation.5 | async-start | bytes 1966080 | tf_op jit(solution)/shard_map/reduce_scatter | solution.py:105
  23.1 0.7 copy-start.3
  23.1 1.0 copy-start.1
  60.6 51.1 %all-to-all-start = ((f32[2,2,192,128]{3,1,0,2:T(2,128)}), f32[2,2,192,128]{3,1,0,2:T(2,128)S(1)}, u32[]{:S(2)}, u32[]{:S(2)}) async-start(f32[2,2,192,128]{3,1,0,2:T(2,128)} %copy.15), calls=%async_computation.1 | async-start | bytes 786432 | tf_op jit(solution)/shard_map/all_to_all | solution.py:114
  111.7 29.7 %all-to-all-start.1 = ((f32[2,2,192,128]{3,1,0,2:T(2,128)}), f32[2,2,192,128]{3,1,0,2:T(2,128)S(1)}, u32[]{:S(2)}, u32[]{:S(2)}) async-start(f32[2,2,192,128]{3,1,0,2:T(2,128)} %copy.17), calls=%async_computation.3 | async-start | bytes 786432 | tf_op jit(solution)/shard_map/all_to_all | solution.py:114
Sparse Core Ops, SparseCore 0:
  16.7 41.6 reduce-scatter.2
  60.9 48.5 reduce-scatter.4

commit v3 on v1

--- a/solution.py
+++ b/solution.py
@@ -88,21 +88,25 @@
     log_weight = jnp.log(beam_weight)
     response = jnp.exp(exponent[:, None, None, None] * log_weight[None])
     stacked = jnp.stack([response * images, response * response])
+    high = lax.reduce_precision(stacked, exponent_bits=8, mantissa_bits=7)
+    rest = stacked - high
+    middle = lax.reduce_precision(rest, exponent_bits=8, mantissa_bits=7)
+    low = rest - middle
+    pieces = jnp.stack([high, middle, low]).astype(jnp.bfloat16)
     row_hit = (
         lax.broadcasted_iota(jnp.int32, (1, MOS_ROWS, side), 1)
         == lax.broadcasted_iota(jnp.int32, (1, MOS_ROWS, side), 2) + offsets[:, 0, None, None]
-    ).astype(jnp.float32)
+    ).astype(jnp.bfloat16)
     col_hit = (
-        lax.broadcasted_iota(jnp.int32, (1, side, MOS_COLS), 2)
-        == lax.broadcasted_iota(jnp.int32, (1, side, MOS_COLS), 1) + offsets[:, 1, None, None]
-    ).astype(jnp.float32)
+        lax.broadcasted_iota(jnp.int32, (1, 1, side, MOS_COLS), 3)
+        == lax.broadcasted_iota(jnp.int32, (1, 1, side, MOS_COLS), 2) + offsets[:, 1, None, None, None]
+    ).astype(jnp.bfloat16)
+    col_hit = jnp.broadcast_to(col_hit, (col_hit.shape[0], 3, side, MOS_COLS))
     rows_placed = jnp.einsum(
-        "bri,acbij->bacrj", row_hit, stacked, precision=lax.Precision.HIGHEST,
-        preferred_element_type=jnp.float32,
+        "bri,pacbij->bpacrj", row_hit, pieces, preferred_element_type=jnp.bfloat16
     )
     planes = jnp.einsum(
-        "bacrj,bjk->acrk", rows_placed, col_hit, precision=lax.Precision.HIGHEST,
-        preferred_element_type=jnp.float32,
+        "bpacrj,bpjk->acrk", rows_placed, col_hit, preferred_element_type=jnp.float32
     )
     own = lax.psum_scatter(planes, "beam", scatter_dimension=3, tiled=True)
     dividend_accumulator = own[0]

time: 140 us -> 142 us (1.014)
  other arithmetic: 2.52 us -> 5.19 us
    another operation x0 -> x1, other arithmetic: none -> 2.03 us
where the time goes in v3:
time: 142 us; the launch traced here: 141 us
  waiting for transfers between devices  94.8 us (67%)
  between operations  13.5 us (10%)
  matrix products  12 us (8%)
  starting transfers between devices  10.5 us (7%)
  local copies, waits for them, and re-layouts  5.34 us (4%)
  other arithmetic  5.19 us (4%)
    reduce_scatter x1, waiting for transfers between devices, local(): own = lax.psum_scatter(planes, 'beam', scatter_dimension=3, tiled=True)  67.1 us
    all_to_all x1, waiting for transfers between devices, local(): lax.all_to_all(jnp.stack([celestial_image, importance_factor]), 'chan', s...  27.7 us
    all_to_all x1, starting transfers between devices, local(): lax.all_to_all(jnp.stack([celestial_image, importance_factor]), 'chan', s...  10.5 us
    dot_general x1, matrix products, local(): jnp.einsum('bpacrj,bpjk->acrk', rows_placed, col_hit, preferred_element_t...  7.57 us
    dot_general x1, matrix products, local(): jnp.einsum('bri,pacbij->bpacrj', row_hit, pieces, preferred_element_type=...  3.19 us
  transfers between devices with their start and end apart: 2, of which 2 were waited for; matrix products, arithmetic and copies ran while one was open for 0% of the time, Pallas kernels for 0%

profile of v3, /device:TPU:65, one launch (start us, length us, event | category | flops | bytes accessed | tf_op | source)
XLA Modules:
  0.0 141.3 jit_solution(9194181677899548509)
XLA Ops:
  6.5 1.3 log.3
  7.8 0.4 multiply_bitcast_fusion
  8.2 0.1 copy-done
  8.4 0.5 multiply_bitcast_fusion.1
  8.9 0.2 copy-done.2
  9.1 0.6 fusion.15
  9.6 2.0 %reduce-precision_convert_fusion.1 = (bf16[1,2,4,9,128,128]{5,4,0,3,2,1:T(8,128)(2,1)S(1)}, bf16[1,2,4,9,128,128]{5,4,0,3,2,1:T(8,128)(2,1)S(1)}, bf16[1,2,4,9,128,128]{5,4,0,3,2,1:T(8,128)(2,1)S(1)}) fusion(f32[1,1,4,9,128,128]{5,4,0,3,2,1:T(8,128)S(1)} %multiply_bitcast_fusion, f32[1,1,4,9,128,128]{5,4,0,3,2,1:T(8,128)S(1)} %multiply_bitcast_fusion.1), kind=kLoop, calls=%fused_computation.11 | loop fusion | flops 9437184 | bytes 11796480 | tf_op jit(solution)/shard_map/convert
  11.7 3.2 %fusion.87 = bf16[9,3,2,4,192,128]{5,4,1,0,3,2:T(8,128)(2,1)S(1)} fusion(bf16[1,2,4,9,128,128]{5,4,0,3,2,1:T(8,128)(2,1)S(1)} %get-tuple-element.20, bf16[1,2,4,9,128,128]{5,4,0,3,2,1:T(8,128)(2,1)S(1)} %get-tuple-element.19, bf16[1,2,4,9,128,128]{5,4,0,3,2,1:T(8,128)(2,1)S(1)} %get-tuple-element.18, s32[9]{0:T(128)S(1)} %get-tuple-element.25), kind=kOutput, calls=%fused_computation.1.clone.clone.clone.2 | convolution fusion | flops 1366474752 | bytes 17694756 | tf_op jit(solution)/shard_map/bri,pacbij->bpacrj/dot_general | solution.py:105
  14.9 7.6 %fusion.16 = f32[2,4,192,512]{3,2,1,0:T(8,128)} fusion(bf16[9,128,512]{2,1,0:T(8,128)(2,1)S(1)} %fusion.15, bf16[9,3,2,4,192,128]{5,4,1,0,3,2:T(8,128)(2,1)S(1)} %fusion.87), kind=kOutput, calls=%fused_computation.18 | convolution fusion | flops 5435817984 | bytes 14942208 | tf_op jit(solution)/shard_map/bpacrj,bpjk->acrk/dot_general | solution.py:108
  22.5 0.7 copy-done.3
  23.2 67.1 %reduce-scatter.2.cloned.1.call-done = f32[2,4,192,128]{3,2,1,0:T(8,128)} async-done(((f32[2,4,192,512]{3,2,1,0:T(8,128)}), f32[2,4,192,128]{3,2,1,0:T(8,128)}) %reduce-scatter.2.cloned.1.call-update) | async-done | bytes 786448 | tf_op jit(solution)/shard_map/reduce_scatter | solution.py:111
  90.3 1.2 fusion.33
  91.6 1.4 copy.14
  93.0 10.5 %all-to-all-start = ((f32[2,4,192,128]{3,1,0,2:T(4,128)}), f32[2,4,192,128]{3,1,0,2:T(4,128)S(1)}, u32[]{:S(2)}, u32[]{:S(2)}) async-start(f32[2,4,192,128]{3,1,0,2:T(4,128)} %copy.14), calls=%async_computation.1 | async-start | bytes 1572864 | tf_op jit(solution)/shard_map/all_to_all | solution.py:122
  103.6 27.7 %all-to-all-done = f32[2,4,192,128]{3,1,0,2:T(4,128)S(1)} async-done(((f32[2,4,192,128]{3,1,0,2:T(4,128)}), f32[2,4,192,128]{3,1,0,2:T(4,128)S(1)}, u32[]{:S(2)}, u32[]{:S(2)}) %all-to-all-start) | async-done | bytes 786464 | tf_op jit(solution)/shard_map/all_to_all | solution.py:122
  131.3 0.1 copy.15
  131.5 0.1 copy.16
  131.7 0.1 copy.17
  131.8 0.3 fusion.27
  132.1 0.3 fusion.29
  132.6 0.7 convolution_subtract_fusion
  133.3 0.1 multiply_add_fusion
  133.4 0.2 copy.18
  133.6 0.9 copy.19
  (25 shorter events, 0.6 us)
Async XLA Ops:
  6.5 1.8 %copy-start = (f32[4,9,128,128]{3,2,1,0:T(8,128)S(1)}, f32[4,9,128,128]{3,2,1,0:T(8,128)}, u32[]{:S(2)}) copy-start(f32[4,9,128,128]{3,2,1,0:T(8,128)} %param.5) | copy-start | bytes 7077892
  6.5 83.7 %reduce-scatter.2.cloned.1.call-start = ((), (), s32[]{:S(2)}) async-start(), calls=%async_computation.2 | async-start | bytes 3932160 | tf_op jit(solution)/shard_map/reduce_scatter | solution.py:111
  8.4 0.7 copy-start.2
  22.4 0.7 copy-start.3
  22.4 67.8 %copy-start.1 = (s32[4,192,128]{2,1,0:T(8,128)S(1)}, s32[4,192,128]{2,1,0:T(8,128)}, u32[]{:S(2)}) copy-start(s32[4,192,128]{2,1,0:T(8,128)} %param.8) | copy-start | bytes 1179652
  93.0 38.3 %all-to-all-start = ((f32[2,4,192,128]{3,1,0,2:T(4,128)}), f32[2,4,192,128]{3,1,0,2:T(4,128)S(1)}, u32[]{:S(2)}, u32[]{:S(2)}) async-start(f32[2,4,192,128]{3,1,0,2:T(4,128)} %copy.14), calls=%async_computation.1 | async-start | bytes 1572864 | tf_op jit(solution)/shard_map/all_to_all | solution.py:122
Sparse Core Ops, SparseCore 0:
  22.6 67.6 reduce-scatter.1

commit v4 on v1

--- a/solution.py
+++ b/solution.py
@@ -4,6 +4,7 @@
 from jax.sharding import PartitionSpec as P
 
 MOS_ROWS = 192
+CHAN = ("xy", "zhi", "core")
 MOS_COLS = 512
 
 
@@ -82,7 +83,7 @@
     ch_dev = images.shape[0]
     side = images.shape[2]
     all_channels = regression_indicator.shape[0]
-    first_channel = lax.axis_index("chan") * ch_dev
+    first_channel = lax.axis_index(CHAN) * ch_dev
     channel_ids = first_channel + jnp.arange(ch_dev, dtype=jnp.int32)
     exponent = 1.0 + 0.5 * channel_ids.astype(jnp.float32) / (all_channels - 1)
     log_weight = jnp.log(beam_weight)
@@ -115,19 +116,29 @@
     importance_factor = normalizer_accumulated * (
         emission_absent[:, None, None] * accepted_entries + 0.01
     )
-    arrived = lax.all_to_all(
-        jnp.stack([celestial_image, importance_factor]), "chan", split_axis=2, concat_axis=1, tiled=True
-    )
-    return clean_pair((arrived[0], arrived[1]))
+    both = jnp.stack([celestial_image, importance_factor])
+    col_dev = both.shape[3]
+    planes_xy = lax.psum(1, "xy")
+    planes_zc = lax.psum(1, ("zhi", "core"))
+    rows_dev = both.shape[2] // (planes_xy * planes_zc)
+    both = both.reshape(2, ch_dev, planes_xy, planes_zc * rows_dev, col_dev)
+    both = lax.all_to_all(both, "xy", split_axis=2, concat_axis=2, tiled=True)
+    both = lax.all_to_all(both, ("zhi", "core"), split_axis=3, concat_axis=3, tiled=True)
+    both = both.reshape(2, ch_dev, planes_xy, planes_zc, rows_dev, col_dev)
+    both = both.transpose(0, 2, 3, 1, 4, 5).reshape(2, all_channels, rows_dev, col_dev)
+    return clean_pair((both[0], both[1]))
 
 
 def solution(mesh):
+    devices = mesh.devices
+    planes = devices.shape[0] // 4
+    split = jax.sharding.Mesh(devices.reshape(planes, 2, 2, devices.shape[1]), ("xy", "zhi", "core", "beam"))
     in_specs = (
-        P("chan", "beam", None, None),
+        P(CHAN, "beam", None, None),
         P("beam", None, None),
         P("beam", None),
-        P("chan", None, "beam"),
+        P(CHAN, None, "beam"),
         P(),
     )
-    out_specs = P(None, "chan", "beam")
-    return jax.shard_map(local, mesh=mesh, in_specs=in_specs, out_specs=out_specs, check_vma=False)
+    out_specs = P(None, CHAN, "beam")
+    return jax.shard_map(local, mesh=split, in_specs=in_specs, out_specs=out_specs, check_vma=False)

time: 140 us -> 151 us (1.079)
  blocking collectives: 0 us -> 19.7 us
  waiting for transfers between devices: 94.8 us -> 89.9 us
  starting transfers between devices: 10.5 us -> 6 us
    all_to_all x0 -> x1, blocking collectives: none -> 19.7 us  [local(): both = lax.all_to_all(both, 'xy', split_axis=2, concat_axis=2, tiled=True)]
    all_to_all x1, waiting for transfers between devices: 27.7 us -> 22.8 us  [local(): lax.all_to_all(both, ('zhi', 'core'), split_axis=3, concat_axis=3, tiled=...]
    all_to_all x1, starting transfers between devices: 10.5 us -> 6 us  [local(): lax.all_to_all(both, ('zhi', 'core'), split_axis=3, concat_axis=3, tiled=...]
where the time goes in v4:
time: 151 us; the launch traced here: 150 us
  waiting for transfers between devices  89.9 us (60%)
  blocking collectives  19.7 us (13%)
  between operations  13.5 us (9%)
  matrix products  12.9 us (9%)
  starting transfers between devices  6 us (4%)
  local copies, waits for them, and re-layouts  5.77 us (4%)
  other arithmetic  2.64 us (2%)
    reduce_scatter x1, waiting for transfers between devices, local(): own = lax.psum_scatter(planes, 'beam', scatter_dimension=3, tiled=True)  67.1 us
    all_to_all x1, waiting for transfers between devices, local(): lax.all_to_all(both, ('zhi', 'core'), split_axis=3, concat_axis=3, tiled=...  22.8 us
    all_to_all x1, blocking collectives, local(): both = lax.all_to_all(both, 'xy', split_axis=2, concat_axis=2, tiled=True)  19.7 us
    dot_general x1, matrix products, local(): jnp.einsum('bacrj,bjk->acrk', rows_placed, col_hit, precision=lax.Precisi...  8.18 us
    all_to_all x1, starting transfers between devices, local(): lax.all_to_all(both, ('zhi', 'core'), split_axis=3, concat_axis=3, tiled=...  6 us
    dot_general x1, matrix products, local(): jnp.einsum('bri,acbij->bacrj', row_hit, stacked, precision=lax.Precision....  3.43 us
  transfers between devices with their start and end apart: 2, of which 2 were waited for; matrix products, arithmetic and copies ran while one was open for 0% of the time, Pallas kernels for 0%

profile of v4, /device:TPU:65, one launch (start us, length us, event | category | flops | bytes accessed | tf_op | source)
XLA Modules:
  0.0 150.4 jit_solution(12270348183312391615)
XLA Ops:
  6.5 1.3 log.3
  7.8 0.4 exponential_multiply_fusion
  8.2 0.1 copy-done
  8.4 0.4 multiply_bitcast_fusion
  8.8 0.3 copy-done.2
  9.1 3.4 %fusion.2 = f32[9,2,4,128,192]{3,4,0,2,1:T(8,128)S(1)} fusion(f32[1,4,9,128,128]{4,3,2,1,0:T(8,128)S(1)} %exponential_multiply_fusion, f32[1,4,9,128,128]{4,3,2,1,0:T(8,128)S(1)} %multiply_bitcast_fusion, s32[9]{0:T(128)S(1)} %get-tuple-element.23), kind=kOutput, calls=%fused_computation.2 | convolution fusion | flops 2719531008 | bytes 11796516 | tf_op jit(solution)/shard_map/bri,acbij->bacrj/dot_general | solution.py:100
  12.5 8.2 %fusion.8 = f32[2,4,192,512]{3,2,1,0:T(8,128)} fusion(f32[9,2,4,128,192]{3,4,0,2,1:T(8,128)S(1)} %fusion.2, s32[9]{0:T(128)S(1)} %get-tuple-element.22), kind=kOutput, calls=%fused_computation.10 | convolution fusion | flops 10872815616 | bytes 10223652 | tf_op jit(solution)/shard_map/bacrj,bjk->acrk/dot_general | solution.py:104
  20.7 0.7 copy-done.3
  21.4 67.1 %reduce-scatter.2.cloned.1.call-done = f32[2,4,192,128]{3,2,1,0:T(8,128)} async-done(((f32[2,4,192,512]{3,2,1,0:T(8,128)}), f32[2,4,192,128]{3,2,1,0:T(8,128)}) %reduce-scatter.2.cloned.1.call-update) | async-done | bytes 786448 | tf_op jit(solution)/shard_map/reduce_scatter | solution.py:108
  88.5 1.2 fusion.22
  89.8 0.3 copy.15
  90.0 0.3 copy.16
  90.3 0.2 pad_maximum_fusion
  90.5 19.7 %all_to_all.10 = f32[2,4,16,12,128]{4,1,3,0,2:T(4,128)S(1)} all-to-all(f32[2,4,16,12,128]{4,1,3,0,2:T(4,128)S(1)} %copy.17), channel_id=1, replica_groups=mesh['xy'=16,'zhi'=2,'core'=2,'beam'=4] {'xy'}, dimensions={2} | all-to-all | bytes 1572864 | tf_op jit(solution)/shard_map/all_to_all | solution.py:125
  110.3 1.1 copy.18
  111.4 6.0 %all-to-all-start.1 = ((f32[2,4,16,12,128]{4,1,2,0,3:T(4,128)}), f32[2,4,16,12,128]{4,1,2,0,3:T(4,128)S(1)}, u32[]{:S(2)}, u32[]{:S(2)}) async-start(f32[2,4,16,12,128]{4,1,2,0,3:T(4,128)} %copy.18), calls=%async_computation.2 | async-start | bytes 1572864 | tf_op jit(solution)/shard_map/all_to_all | solution.py:126
  117.5 22.8 %all-to-all-done.1 = f32[2,4,16,12,128]{4,1,2,0,3:T(4,128)S(1)} async-done(((f32[2,4,16,12,128]{4,1,2,0,3:T(4,128)}), f32[2,4,16,12,128]{4,1,2,0,3:T(4,128)S(1)}, u32[]{:S(2)}, u32[]{:S(2)}) %all-to-all-start.1) | async-done | bytes 786464 | tf_op jit(solution)/shard_map/all_to_all | solution.py:126
  140.5 0.2 copy.20
  140.7 0.2 copy.21
  140.9 0.3 fusion.17
  141.2 0.3 fusion.19
  141.7 0.7 convolution_subtract_fusion
  142.5 0.2 copy.22
  142.7 0.9 copy.23
  (27 shorter events, 0.8 us)
Async XLA Ops:
  6.5 1.8 %copy-start = (f32[4,9,128,128]{3,2,1,0:T(8,128)S(1)}, f32[4,9,128,128]{3,2,1,0:T(8,128)}, u32[]{:S(2)}) copy-start(f32[4,9,128,128]{3,2,1,0:T(8,128)} %param.5) | copy-start | bytes 7077892
  6.5 82.0 %reduce-scatter.2.cloned.1.call-start = ((), (), s32[]{:S(2)}) async-start(), calls=%async_computation.3 | async-start | bytes 3932160 | tf_op jit(solution)/shard_map/reduce_scatter | solution.py:108
  8.4 0.7 copy-start.2
  20.7 0.7 copy-start.3
  20.7 67.8 %copy-start.1 = (s32[4,192,128]{2,1,0:T(8,128)S(1)}, s32[4,192,128]{2,1,0:T(8,128)}, u32[]{:S(2)}) copy-start(s32[4,192,128]{2,1,0:T(8,128)} %param.8) | copy-start | bytes 1179652
  111.4 29.0 %all-to-all-start.1 = ((f32[2,4,16,12,128]{4,1,2,0,3:T(4,128)}), f32[2,4,16,12,128]{4,1,2,0,3:T(4,128)S(1)}, u32[]{:S(2)}, u32[]{:S(2)}) async-start(f32[2,4,16,12,128]{4,1,2,0,3:T(4,128)} %copy.18), calls=%async_computation.2 | async-start | bytes 1572864 | tf_op jit(solution)/shard_map/all_to_all | solution.py:126
Sparse Core Ops, SparseCore 0:
  20.8 67.6 reduce-scatter.1

commit v5 on v1

--- a/solution.py
+++ b/solution.py
@@ -2,6 +2,7 @@
 import jax.numpy as jnp
 from jax import lax
 from jax.sharding import PartitionSpec as P
+
 
 MOS_ROWS = 192
 MOS_COLS = 512
@@ -78,7 +79,86 @@
     return smoothed.reshape(channels, rows, columns)
 
 
-def local(images, beam_weight, offsets, rejected_indicator, regression_indicator):
+JITTER = 16
+
+
+def covered_rows(groups, per_group, side):
+    grid = int(round((groups * per_group) ** 0.5))
+    block = MOS_COLS // groups
+
+    def span(base, inner, top):
+        return (max(base - JITTER, 0), min(base + JITTER, top)) if inner else (base, base)
+
+    cover = {}
+    for group in range(groups):
+        for target in range(groups):
+            rows = None
+            for index in range(per_group):
+                beam = group * per_group + index
+                row, col = beam // grid, beam % grid
+                row_lo, row_hi = span(row * (MOS_ROWS - side) // (grid - 1), 0 < row < grid - 1, MOS_ROWS - side)
+                col_lo, col_hi = span(col * (MOS_COLS - side) // (grid - 1), 0 < col < grid - 1, MOS_COLS - side)
+                if col_lo < block * (target + 1) and col_hi + side > block * target:
+                    low, high = row_lo, row_hi + side
+                    rows = (low, high) if rows is None else (min(rows[0], low), max(rows[1], high))
+            cover[group, target] = rows
+    return cover
+
+
+def join(first, second):
+    if first is None:
+        return second
+    if second is None:
+        return first
+    return (min(first[0], second[0]), max(first[1], second[1]))
+
+
+def step_windows(cover, groups, rightward):
+    windows = []
+    for step in range(1, groups):
+        window = None
+        senders = range(step) if rightward else range(groups - step, groups)
+        for sender in senders:
+            target = sender + groups - step if rightward else sender - groups + step
+            contributors = range(sender + 1) if rightward else range(sender, groups)
+            for contributor in contributors:
+                window = join(window, cover[contributor, target])
+        low = (window[0] // 8) * 8
+        high = min(-(-window[1] // 8) * 8, MOS_ROWS)
+        windows.append((low, high))
+    return windows
+
+
+def line_reduce_scatter(planes, per_group, side):
+    groups = lax.psum(1, "beam")
+    block = MOS_COLS // groups
+    me = lax.axis_index("beam")
+    cover = covered_rows(groups, per_group, side)
+    total = lax.dynamic_slice_in_dim(planes, me * block, block, 3)
+    for rightward in (True, False):
+        windows = step_windows(cover, groups, rightward)
+        carried = None
+        for step, (low, high) in enumerate(windows, start=1):
+            target = me + groups - step if rightward else me - groups + step
+            target = jnp.clip(target, 0, groups - 1)
+            piece = lax.dynamic_slice(
+                planes, (0, 0, low, target * block), planes.shape[:2] + (high - low, block)
+            )
+            if carried is not None:
+                before_low, before_high = windows[step - 2]
+                piece = piece.at[:, :, before_low - low : before_high - low].add(carried)
+            pairs = (
+                [(i, i + 1) for i in range(step)]
+                if rightward
+                else [(i, i - 1) for i in range(groups - step, groups)]
+            )
+            carried = lax.ppermute(piece, "beam", pairs)
+        low, high = windows[-1]
+        total = total.at[:, :, low:high].add(carried)
+    return total
+
+
+def local_body(images, beam_weight, offsets, rejected_indicator, regression_indicator):
     ch_dev = images.shape[0]
     side = images.shape[2]
     all_channels = regression_indicator.shape[0]
@@ -88,13 +168,17 @@
     log_weight = jnp.log(beam_weight)
     response = jnp.exp(exponent[:, None, None, None] * log_weight[None])
     stacked = jnp.stack([response * images, response * response])
+    side_rows = MOS_ROWS - side
+    side_cols = MOS_COLS - side
+    row_start = jnp.clip(offsets[:, 0], 0, side_rows)
+    col_start = jnp.clip(offsets[:, 1], 0, side_cols)
     row_hit = (
         lax.broadcasted_iota(jnp.int32, (1, MOS_ROWS, side), 1)
-        == lax.broadcasted_iota(jnp.int32, (1, MOS_ROWS, side), 2) + offsets[:, 0, None, None]
+        == lax.broadcasted_iota(jnp.int32, (1, MOS_ROWS, side), 2) + row_start[:, None, None]
     ).astype(jnp.float32)
     col_hit = (
         lax.broadcasted_iota(jnp.int32, (1, side, MOS_COLS), 2)
-        == lax.broadcasted_iota(jnp.int32, (1, side, MOS_COLS), 1) + offsets[:, 1, None, None]
+        == lax.broadcasted_iota(jnp.int32, (1, side, MOS_COLS), 1) + col_start[:, None, None]
     ).astype(jnp.float32)
     rows_placed = jnp.einsum(
         "bri,acbij->bacrj", row_hit, stacked, precision=lax.Precision.HIGHEST,
@@ -104,7 +188,7 @@
         "bacrj,bjk->acrk", rows_placed, col_hit, precision=lax.Precision.HIGHEST,
         preferred_element_type=jnp.float32,
     )
-    own = lax.psum_scatter(planes, "beam", scatter_dimension=3, tiled=True)
+    own = line_reduce_scatter(planes, images.shape[1], side)
     dividend_accumulator = own[0]
     normalizer_accumulated = own[1]
     accepted_entries = 1.0 - rejected_indicator.astype(jnp.float32)
@@ -130,4 +214,4 @@
         P(),
     )
     out_specs = P(None, "chan", "beam")
-    return jax.shard_map(local, mesh=mesh, in_specs=in_specs, out_specs=out_specs, check_vma=False)
+    return jax.shard_map(local_body, mesh=mesh, in_specs=in_specs, out_specs=out_specs, check_vma=False)

time: 140 us -> 149 us (1.064); the launches traced: 140 us -> 147 us
  starting transfers between devices: 10.5 us -> 27.6 us
  between operations: 13.5 us -> 0.28 us
  waiting for transfers between devices: 94.8 us -> 82.4 us
  other arithmetic: 2.52 us -> 14.6 us
  local copies, waits for them, and re-layouts: 5.43 us -> 8.72 us
    reduce_scatter x1 -> x0, waiting for transfers between devices: 67.1 us -> none  [local(): own = lax.psum_scatter(planes, 'beam', scatter_dimension=3, tiled=True)]
    ppermute x0 -> x6, waiting for transfers between devices: none -> 55 us  [line_reduce_scatter(): carried = lax.ppermute(piece, 'beam', pairs)]
    scatter-add x0 -> x6, other arithmetic: none -> 11.8 us  [the longest x4 9.1 us: line_reduce_scatter(): piece = piece.at[:, :, before_low - low:before_high - low].add(carried)]
    ppermute x0 -> x6, starting transfers between devices: none -> 11.2 us  [line_reduce_scatter(): carried = lax.ppermute(piece, 'beam', pairs)]
    all_to_all x1, starting transfers between devices: 10.5 us -> 16.4 us  [local_body(): lax.all_to_all(jnp.stack([celestial_image, importance_factor]), 'chan', s...]
    dynamic_slice x0 -> x4, local copies, waits for them, and re-layouts: none -> 3.29 us  [the longest x3 3.18 us: line_reduce_scatter(): lax.dynamic_slice(planes, (0, 0, low, target * block), planes.shape[:2] +...]
  transfers between devices with their start and end apart: 2 -> 7, of which waited for: 2 -> 6; matrix products, arithmetic and copies ran while one was open for 0% -> 4% of each run, Pallas kernels for 0% -> 0%
where the time goes in v5:
time: 149 us; the launch traced here: 147 us
  waiting for transfers between devices  82.4 us (55%)
  starting transfers between devices  27.6 us (19%)
  other arithmetic  14.6 us (10%)
  matrix products  12.9 us (9%)
  local copies, waits for them, and re-layouts  8.72 us (6%)
    ppermute x6, waiting for transfers between devices, line_reduce_scatter(): carried = lax.ppermute(piece, 'beam', pairs)  55 us
    all_to_all x1, waiting for transfers between devices, local_body(): lax.all_to_all(jnp.stack([celestial_image, importance_factor]), 'chan', s...  27.4 us
    all_to_all x1, starting transfers between devices, local_body(): lax.all_to_all(jnp.stack([celestial_image, importance_factor]), 'chan', s...  16.4 us
    ppermute x6, starting transfers between devices, line_reduce_scatter(): carried = lax.ppermute(piece, 'beam', pairs)  11.2 us
    scatter-add x4, other arithmetic, line_reduce_scatter(): piece = piece.at[:, :, before_low - low:before_high - low].add(carried)  9.1 us
    dot_general x1, matrix products, local_body(): jnp.einsum('bacrj,bjk->acrk', rows_placed, col_hit, precision=lax.Precisi...  6.53 us
    dot_general x1, matrix products, local_body(): jnp.einsum('bri,acbij->bacrj', row_hit, stacked, precision=lax.Precision....  5.11 us
    dynamic_slice x3, local copies, waits for them, and re-layouts, line_reduce_scatter(): lax.dynamic_slice(planes, (0, 0, low, target * block), planes.shape[:2] +...  3.18 us
  transfers between devices with their start and end apart: 7, of which 6 were waited for; matrix products, arithmetic and copies ran while one was open for 4% of the time, Pallas kernels for 0%

profile of v5, /device:TPU:65, one launch (start us, length us, event | category | flops | bytes accessed | tf_op | source)
XLA Modules:
  0.0 146.5 jit_solution(9120372516398868264)
XLA Ops:
  1.6 1.3 copy-done
  2.8 1.8 %multiply_bitcast_fusion = f32[1,4,9,128,128]{4,3,2,1,0:T(8,128)} fusion(f32[4,9,128,128]{3,2,1,0:T(8,128)S(1)} %copy-done, f32[9,128,128]{2,1,0:T(8,128)S(1)} %log.3, f32[4]{0:T(128)S(1)} %multiply_add_fusion.3), kind=kLoop, calls=%fused_computation.8 | loop fusion | flops 1179648 | bytes 5308432 | tf_op jit(solution)/shard_map/stack | solution.py:170
  4.7 5.1 %fusion.2 = f32[9,2,4,128,192]{3,4,0,2,1:T(8,128)S(1)} fusion(f32[1,4,9,128,128]{4,3,2,1,0:T(8,128)S(1)} %exponential_multiply_fusion, f32[1,4,9,128,128]{4,3,2,1,0:T(8,128)} %multiply_bitcast_fusion, s32[9]{0:T(128)S(1)} %get-tuple-element.101), kind=kOutput, calls=%fused_computation.2 | convolution fusion | flops 2719531008 | bytes 11796516 | tf_op jit(solution)/shard_map/bri,acbij->bacrj/dot_general | solution.py:183
  9.8 6.5 %fusion.8 = f32[2,4,192,512]{3,2,1,0:T(8,128)S(1)} fusion(f32[9,2,4,128,192]{3,4,0,2,1:T(8,128)S(1)} %fusion.2, s32[9]{0:T(128)S(1)} %get-tuple-element.100), kind=kOutput, calls=%fused_computation.10 | convolution fusion | flops 10872815616 | bytes 10223652 | tf_op jit(solution)/shard_map/bacrj,bjk->acrk/dot_general | solution.py:187
  17.2 1.3 collective-permute-start.3
  19.5 12.7 %collective-permute-done.3 = f32[2,4,128,128]{3,2,1,0:T(8,128)} collective-permute-done((f32[2,4,128,128]{3,2,1,0:T(8,128)}, f32[2,4,128,128]{3,2,1,0:T(8,128)}, u32[]{:S(2)}, u32[]{:S(2)}) %collective-permute-start.3) | collective-permute-done | bytes 524320 | tf_op jit(solution)/shard_map/ppermute | solution.py:155
  32.2 2.3 %add_dynamic-update-slice_fusion.3 = (f32[2,4,176,128]{3,2,1,0:T(8,128)}, f32[2,4,128,128]{3,2,1,0:T(8,128)}) fusion(f32[2,4,176,128]{3,2,1,0:T(8,128)} %constant_dynamic-slice_fusion, f32[2,4,128,128]{3,2,1,0:T(8,128)} %collective-permute-done.3, f32[2,4,192,512]{3,2,1,0:T(8,128)S(1)} %fusion.8, s32[]{:T(128)S(6)} %select_n.44, s32[]{:T(128)S(6)} %select_n.40), kind=kLoop, calls=%fused_computation.21 | loop fusion | flops 131072 | bytes 2621448 | tf_op jit(solution)/shard_map/scatter-add | solution.py:149
  34.5 1.9 %collective-permute-start.4 = (f32[2,4,176,128]{3,2,1,0:T(8,128)}, f32[2,4,176,128]{3,2,1,0:T(8,128)}, u32[]{:S(2)}, u32[]{:S(2)}) collective-permute-start(f32[2,4,176,128]{3,2,1,0:T(8,128)} %get-tuple-element.92), channel_id=1, source_target_pairs={{2,1},{3,2},{6,5},{7,6},{10,9},{11,10},{14,13},{15,14},{18,17},{19... | collective-permute-start | bytes 2162696 | tf_op jit(solution)/shard_map/ppermute | solution.py:155
  36.4 1.5 collective-permute-start
  37.8 1.3 constant_dynamic-slice_fusion.1
  39.2 13.6 %collective-permute-done.4 = f32[2,4,176,128]{3,2,1,0:T(8,128)} collective-permute-done((f32[2,4,176,128]{3,2,1,0:T(8,128)}, f32[2,4,176,128]{3,2,1,0:T(8,128)}, u32[]{:S(2)}, u32[]{:S(2)}) %collective-permute-start.4) | collective-permute-done | bytes 720928 | tf_op jit(solution)/shard_map/ppermute | solution.py:155
  52.8 2.5 %add_dynamic-update-slice_fusion.1 = (f32[2,4,184,128]{3,2,1,0:T(8,128)}, f32[2,4,176,128]{3,2,1,0:T(8,128)}) fusion(f32[2,4,184,128]{3,2,1,0:T(8,128)} %get-tuple-element.94, f32[2,4,176,128]{3,2,1,0:T(8,128)} %collective-permute-done.4, f32[2,4,192,512]{3,2,1,0:T(8,128)S(1)} %fusion.8, s32[]{:T(128)S(6)} %select_n.42, s32[]{:T(128)S(6)} %select_n.38), kind=kLoop, calls=%fused_computation.19 | loop fusion | flops 180224 | bytes 3604488 | tf_op jit(solution)/shard_map/scatter-add | solution.py:149
  55.3 2.1 %add_dynamic-update-slice_fusion.4 = f32[2,4,176,128]{3,2,1,0:T(8,128)} fusion(f32[2,4,176,128]{3,2,1,0:T(8,128)} %get-tuple-element.91, f32[2,4,128,128]{3,2,1,0:T(8,128)} %collective-permute-done, f32[2,4,192,512]{3,2,1,0:T(8,128)S(1)} %fusion.8, s32[]{:T(128)S(6)} %select_n.39), kind=kLoop, calls=%fused_computation.22 | loop fusion | flops 131072 | bytes 1572868 | tf_op jit(solution)/shard_map/scatter-add | solution.py:149
  57.4 1.3 collective-permute-start.1
  58.7 16.2 %collective-permute-done.1 = f32[2,4,176,128]{3,2,1,0:T(8,128)} collective-permute-done((f32[2,4,176,128]{3,2,1,0:T(8,128)}, f32[2,4,176,128]{3,2,1,0:T(8,128)}, u32[]{:S(2)}, u32[]{:S(2)}) %collective-permute-start.1) | collective-permute-done | bytes 720928 | tf_op jit(solution)/shard_map/ppermute | solution.py:155
  74.9 2.3 %add_dynamic-update-slice_fusion.2 = f32[2,4,184,128]{3,2,1,0:T(8,128)} fusion(f32[2,4,184,128]{3,2,1,0:T(8,128)} %get-tuple-element.95, f32[2,4,176,128]{3,2,1,0:T(8,128)} %collective-permute-done.1, f32[2,4,192,512]{3,2,1,0:T(8,128)S(1)} %fusion.8, s32[]{:T(128)S(6)} %select_n.37), kind=kLoop, calls=%fused_computation.20 | loop fusion | flops 180224 | bytes 2162692 | tf_op jit(solution)/shard_map/scatter-add | solution.py:149
  77.2 1.9 %collective-permute-start.2 = (f32[2,4,184,128]{3,2,1,0:T(8,128)}, f32[2,4,184,128]{3,2,1,0:T(8,128)}, u32[]{:S(2)}, u32[]{:S(2)}) collective-permute-start(f32[2,4,184,128]{3,2,1,0:T(8,128)} %add_dynamic-update-slice_fusion.2), channel_id=1, source_target_pairs={{0,1},{1,2},{2,3},{4,5},{5,6},{6,7},{8,9},{9,10},{10,11},{12,13},{... | collective-permute-start | bytes 2261000 | tf_op jit(solution)/shard_map/ppermute | solution.py:155
  79.1 3.4 %collective-permute-start.5 = (f32[2,4,184,128]{3,2,1,0:T(8,128)}, f32[2,4,184,128]{3,2,1,0:T(8,128)}, u32[]{:S(2)}, u32[]{:S(2)}) collective-permute-start(f32[2,4,184,128]{3,2,1,0:T(8,128)} %get-tuple-element.90), channel_id=1, source_target_pairs={{1,0},{2,1},{3,2},{5,4},{6,5},{7,6},{9,8},{10,9},{11,10},{13,12},{... | collective-permute-start | bytes 2261000 | tf_op jit(solution)/shard_map/ppermute | solution.py:155
  82.7 11.8 %collective-permute-done.2 = f32[2,4,184,128]{3,2,1,0:T(8,128)} collective-permute-done((f32[2,4,184,128]{3,2,1,0:T(8,128)}, f32[2,4,184,128]{3,2,1,0:T(8,128)}, u32[]{:S(2)}, u32[]{:S(2)}) %collective-permute-start.2) | collective-permute-done | bytes 753696 | tf_op jit(solution)/shard_map/ppermute | solution.py:155
  94.5 1.4 add_dynamic-update-slice_fusion
  96.4 1.3 fusion.16
  97.9 1.4 copy.14
  99.3 16.4 %all-to-all-start = ((f32[2,4,192,128]{3,1,0,2:T(4,128)}), f32[2,4,192,128]{3,1,0,2:T(4,128)S(1)}, u32[]{:S(2)}, u32[]{:S(2)}) async-start(f32[2,4,192,128]{3,1,0,2:T(4,128)} %copy.14), calls=%async_computation | async-start | bytes 1572864 | tf_op jit(solution)/shard_map/all_to_all | solution.py:202
  115.9 27.4 %all-to-all-done = f32[2,4,192,128]{3,1,0,2:T(4,128)S(1)} async-done(((f32[2,4,192,128]{3,1,0,2:T(4,128)}), f32[2,4,192,128]{3,1,0,2:T(4,128)S(1)}, u32[]{:S(2)}, u32[]{:S(2)}) %all-to-all-start) | async-done | bytes 786464 | tf_op jit(solution)/shard_map/all_to_all | solution.py:202
  (42 shorter events, 7.5 us)
Async XLA Ops:
  1.2 1.7 %copy-start = (f32[4,9,128,128]{3,2,1,0:T(8,128)S(1)}, f32[4,9,128,128]{3,2,1,0:T(8,128)}, u32[]{:S(2)}) copy-start(f32[4,9,128,128]{3,2,1,0:T(8,128)} %param.17) | copy-start | bytes 7077892
  2.8 1.8 %copy-start.2 = (s32[9,2]{0,1:T(2,128)S(1)}, s32[9,2]{0,1:T(2,128)}, u32[]{:S(2)}) copy-start(s32[9,2]{0,1:T(2,128)} %param.19) | copy-start | bytes 220
  17.2 15.0 %collective-permute-start.3 = (f32[2,4,128,128]{3,2,1,0:T(8,128)}, f32[2,4,128,128]{3,2,1,0:T(8,128)}, u32[]{:S(2)}, u32[]{:S(2)}) collective-permute-start(f32[2,4,128,128]{3,2,1,0:T(8,128)} %constant_dynamic-slice_fusion.3), channel_id=1, source_target_pairs={{3,2},{7,6},{11,10},{15,14},{19,18},{23,22},{27,26},{31,30},{35,34... | collective-permute-start | bytes 1572872 | tf_op jit(solution)/shard_map/ppermute | solution.py:155
  34.5 18.4 %collective-permute-start.4 = (f32[2,4,176,128]{3,2,1,0:T(8,128)}, f32[2,4,176,128]{3,2,1,0:T(8,128)}, u32[]{:S(2)}, u32[]{:S(2)}) collective-permute-start(f32[2,4,176,128]{3,2,1,0:T(8,128)} %get-tuple-element.92), channel_id=1, source_target_pairs={{2,1},{3,2},{6,5},{7,6},{10,9},{11,10},{14,13},{15,14},{18,17},{19... | collective-permute-start | bytes 2162696 | tf_op jit(solution)/shard_map/ppermute | solution.py:155
  36.4 19.0 %collective-permute-start = (f32[2,4,128,128]{3,2,1,0:T(8,128)}, f32[2,4,128,128]{3,2,1,0:T(8,128)}, u32[]{:S(2)}, u32[]{:S(2)}) collective-permute-start(f32[2,4,128,128]{3,2,1,0:T(8,128)} %get-tuple-element.93), channel_id=1, source_target_pairs={{0,1},{4,5},{8,9},{12,13},{16,17},{20,21},{24,25},{28,29},{32,33},... | collective-permute-start | bytes 1572872 | tf_op jit(solution)/shard_map/ppermute | solution.py:155
  55.3 27.1 %copy-start.3 = (s32[256]{0:T(256)S(1)}, s32[256]{0:T(256)}, u32[]{:S(2)}) copy-start(s32[256]{0:T(256)} %param.21) | copy-start | bytes 3076
  57.4 17.5 %collective-permute-start.1 = (f32[2,4,176,128]{3,2,1,0:T(8,128)}, f32[2,4,176,128]{3,2,1,0:T(8,128)}, u32[]{:S(2)}, u32[]{:S(2)}) collective-permute-start(f32[2,4,176,128]{3,2,1,0:T(8,128)} %add_dynamic-update-slice_fusion.4), channel_id=1, source_target_pairs={{0,1},{1,2},{4,5},{5,6},{8,9},{9,10},{12,13},{13,14},{16,17},{17,1... | collective-permute-start | bytes 2162696 | tf_op jit(solution)/shard_map/ppermute | solution.py:155
  77.2 17.3 %collective-permute-start.2 = (f32[2,4,184,128]{3,2,1,0:T(8,128)}, f32[2,4,184,128]{3,2,1,0:T(8,128)}, u32[]{:S(2)}, u32[]{:S(2)}) collective-permute-start(f32[2,4,184,128]{3,2,1,0:T(8,128)} %add_dynamic-update-slice_fusion.2), channel_id=1, source_target_pairs={{0,1},{1,2},{2,3},{4,5},{5,6},{6,7},{8,9},{9,10},{10,11},{12,13},{... | collective-permute-start | bytes 2261000 | tf_op jit(solution)/shard_map/ppermute | solution.py:155
  79.1 17.4 %collective-permute-start.5 = (f32[2,4,184,128]{3,2,1,0:T(8,128)}, f32[2,4,184,128]{3,2,1,0:T(8,128)}, u32[]{:S(2)}, u32[]{:S(2)}) collective-permute-start(f32[2,4,184,128]{3,2,1,0:T(8,128)} %get-tuple-element.90), channel_id=1, source_target_pairs={{1,0},{2,1},{3,2},{5,4},{6,5},{7,6},{9,8},{10,9},{11,10},{13,12},{... | collective-permute-start | bytes 2261000 | tf_op jit(solution)/shard_map/ppermute | solution.py:155
  82.7 15.1 %copy-start.1 = (s32[4,192,128]{2,1,0:T(8,128)S(1)}, s32[4,192,128]{2,1,0:T(8,128)}, u32[]{:S(2)}) copy-start(s32[4,192,128]{2,1,0:T(8,128)} %param.20) | copy-start | bytes 1179652
  99.3 44.0 %all-to-all-start = ((f32[2,4,192,128]{3,1,0,2:T(4,128)}), f32[2,4,192,128]{3,1,0,2:T(4,128)S(1)}, u32[]{:S(2)}, u32[]{:S(2)}) async-start(f32[2,4,192,128]{3,1,0,2:T(4,128)} %copy.14), calls=%async_computation | async-start | bytes 1572864 | tf_op jit(solution)/shard_map/all_to_all | solution.py:202

commit v6 on v1

--- a/solution.py
+++ b/solution.py
@@ -78,35 +78,62 @@
     return smoothed.reshape(channels, rows, columns)
 
 
+def place(values, row_start, col_start, side, columns, first_column):
+    row_hit = (
+        lax.broadcasted_iota(jnp.int32, (1, MOS_ROWS, side), 1)
+        == lax.broadcasted_iota(jnp.int32, (1, MOS_ROWS, side), 2) + row_start[:, None, None]
+    ).astype(jnp.float32)
+    col_hit = (
+        lax.broadcasted_iota(jnp.int32, (1, side, columns), 2) + first_column
+        == lax.broadcasted_iota(jnp.int32, (1, side, columns), 1) + col_start[:, None, None]
+    ).astype(jnp.float32)
+    rows_placed = jnp.einsum(
+        "bri,cbij->bcrj", row_hit, values, precision=lax.Precision.HIGHEST,
+        preferred_element_type=jnp.float32,
+    )
+    return jnp.einsum(
+        "bcrj,bjk->crk", rows_placed, col_hit, precision=lax.Precision.HIGHEST,
+        preferred_element_type=jnp.float32,
+    )
+
+
 def local(images, beam_weight, offsets, rejected_indicator, regression_indicator):
     ch_dev = images.shape[0]
     side = images.shape[2]
+    col_dev = rejected_indicator.shape[2]
     all_channels = regression_indicator.shape[0]
     first_channel = lax.axis_index("chan") * ch_dev
     channel_ids = first_channel + jnp.arange(ch_dev, dtype=jnp.int32)
     exponent = 1.0 + 0.5 * channel_ids.astype(jnp.float32) / (all_channels - 1)
+    row_start = jnp.clip(offsets[:, 0], 0, MOS_ROWS - side)
+    col_start = jnp.clip(offsets[:, 1], 0, MOS_COLS - side)
     log_weight = jnp.log(beam_weight)
+
+    core = lax.axis_index("chan") % 2
+    half = side // 2
+    own_half = lax.dynamic_slice_in_dim(log_weight, core * half, half, 1)
+    corner = jnp.zeros((log_weight.shape[0], 8, side), jnp.float32)
+    corner = corner.at[:, 0, 0].set(row_start.astype(jnp.float32))
+    corner = corner.at[:, 0, 1].set(col_start.astype(jnp.float32))
+    shared = lax.all_gather(jnp.concatenate([own_half, corner], axis=1), "beam", axis=0, tiled=True)
+    chan_size = lax.psum(1, "chan")
+    other = lax.ppermute(shared, "chan", [(a, a ^ 1) for a in range(chan_size)])
+    first_half = jnp.where(core == 0, shared, other)
+    second_half = jnp.where(core == 0, other, shared)
+    every_log = jnp.concatenate([first_half[:, :half], second_half[:, :half]], axis=1)
+    every_row = first_half[:, half, 0].astype(jnp.int32)
+    every_col = first_half[:, half, 1].astype(jnp.int32)
+
     response = jnp.exp(exponent[:, None, None, None] * log_weight[None])
-    stacked = jnp.stack([response * images, response * response])
-    row_hit = (
-        lax.broadcasted_iota(jnp.int32, (1, MOS_ROWS, side), 1)
-        == lax.broadcasted_iota(jnp.int32, (1, MOS_ROWS, side), 2) + offsets[:, 0, None, None]
-    ).astype(jnp.float32)
-    col_hit = (
-        lax.broadcasted_iota(jnp.int32, (1, side, MOS_COLS), 2)
-        == lax.broadcasted_iota(jnp.int32, (1, side, MOS_COLS), 1) + offsets[:, 1, None, None]
-    ).astype(jnp.float32)
-    rows_placed = jnp.einsum(
-        "bri,acbij->bacrj", row_hit, stacked, precision=lax.Precision.HIGHEST,
-        preferred_element_type=jnp.float32,
+    numerator = place(response * images, row_start, col_start, side, MOS_COLS, 0)
+    dividend_accumulator = lax.psum_scatter(numerator, "beam", scatter_dimension=2, tiled=True)
+
+    every_response = jnp.exp(exponent[:, None, None, None] * every_log[None])
+    col_first = lax.axis_index("beam") * col_dev
+    normalizer_accumulated = place(
+        every_response * every_response, every_row, every_col, side, col_dev, col_first
     )
-    planes = jnp.einsum(
-        "bacrj,bjk->acrk", rows_placed, col_hit, precision=lax.Precision.HIGHEST,
-        preferred_element_type=jnp.float32,
-    )
-    own = lax.psum_scatter(planes, "beam", scatter_dimension=3, tiled=True)
-    dividend_accumulator = own[0]
-    normalizer_accumulated = own[1]
+
     accepted_entries = 1.0 - rejected_indicator.astype(jnp.float32)
     emission_absent = lax.dynamic_slice_in_dim(regression_indicator, first_channel, ch_dev).astype(
         jnp.float32

time: 140 us -> 153 us (1.093)
  matrix products: 12.9 us -> 29.8 us
  waiting for transfers between devices: 94.8 us -> 87.6 us
    reduce_scatter x1, waiting for transfers between devices: 67.1 us -> 25.4 us  [local(): lax.psum_scatter(numerator, 'beam', scatter_dimension=2, tiled=True)]
    all_gather x0 -> x1, waiting for transfers between devices: none -> 31.6 us  [local(): lax.all_gather(jnp.concatenate([own_half, corner], axis=1), 'beam', axis=...]
    dot_general x2 -> x4, matrix products: 11.6 us -> 28.5 us  [the longest x2 14.8 us: place(): jnp.einsum('bcrj,bjk->crk', rows_placed, col_hit, precision=lax.Precision...]
    ppermute x0 -> x1, waiting for transfers between devices: none -> 2.81 us  [local(): other = lax.ppermute(shared, 'chan', [(a, a ^ 1) for a in range(chan_size)])]
  transfers between devices with their start and end apart: 2 -> 4, of which waited for: 2 -> 4; matrix products, arithmetic and copies ran while one was open for 0% -> 14% of each run, Pallas kernels for 0% -> 0%
where the time goes in v6:
time: 153 us
  waiting for transfers between devices  87.6 us (57%)
  matrix products  29.8 us (19%)
  between operations  13.6 us (9%)
  starting transfers between devices  11.4 us (7%)
  local copies, waits for them, and re-layouts  6.56 us (4%)
  other arithmetic  3.96 us (3%)
    all_gather x1, waiting for transfers between devices, local(): lax.all_gather(jnp.concatenate([own_half, corner], axis=1), 'beam', axis=...  31.6 us
    all_to_all x1, waiting for transfers between devices, local(): lax.all_to_all(jnp.stack([celestial_image, importance_factor]), 'chan', s...  27.7 us
    reduce_scatter x1, waiting for transfers between devices, local(): lax.psum_scatter(numerator, 'beam', scatter_dimension=2, tiled=True)  25.4 us
    dot_general x2, matrix products, place(): jnp.einsum('bcrj,bjk->crk', rows_placed, col_hit, precision=lax.Precision...  14.8 us
    dot_general x2, matrix products, place(): jnp.einsum('bri,cbij->bcrj', row_hit, values, precision=lax.Precision.HIG...  13.8 us
    all_to_all x1, starting transfers between devices, local(): lax.all_to_all(jnp.stack([celestial_image, importance_factor]), 'chan', s...  10.5 us
  transfers between devices with their start and end apart: 4, of which 4 were waited for; matrix products, arithmetic and copies ran while one was open for 14% of the time, Pallas kernels for 0%

profile of v6, /device:TPU:65, one launch (start us, length us, event | category | flops | bytes accessed | tf_op | source)
XLA Modules:
  0.0 152.9 jit_solution(11954396857030517619)
XLA Ops:
  6.5 1.3 log.3
  7.8 0.8 fusion.76
  8.6 0.6 fusion.83
  9.2 1.2 scatter.9
  10.5 0.2 copy.16
  10.7 0.8 pad_maximum_fusion.2
  11.5 2.3 %fusion.12 = f32[9,4,128,192]{2,3,0,1:T(8,128)S(1)} fusion(f32[4,9,128,128]{3,2,1,0:T(8,128)S(1)} %copy-done.1, f32[9,128,128]{2,1,0:T(8,128)S(1)} %log.3, f32[4]{0:T(128)S(1)} %multiply_add_fusion.3, s32[9]{0:T(128)S(1)} %get-tuple-element.51), kind=kOutput, calls=%fused_computation.15 | convolution fusion | flops 1360576512 | bytes 6488116 | tf_op jit(solution)/shard_map/bri,cbij->bcrj/dot_general | solution.py:90
  13.9 4.6 %fusion.21 = f32[4,192,512]{2,1,0:T(8,128)} fusion(f32[9,4,128,192]{2,3,0,1:T(8,128)S(1)} %fusion.12, s32[9]{0:T(128)S(1)} %get-tuple-element.48), kind=kOutput, calls=%fused_computation.22 | convolution fusion | flops 5436997632 | bytes 5111844 | tf_op jit(solution)/shard_map/bcrj,bjk->crk/dot_general | solution.py:94
  18.5 31.6 %all-gather.2.cloned.1.call-done = f32[36,72,128]{2,1,0:T(8,128)} async-done(((f32[9,72,128]{2,1,0:T(8,128)}), f32[36,72,128]{2,1,0:T(8,128)}) %all-gather.2.cloned.1.call-update) | async-done | bytes 1327120 | tf_op jit(solution)/shard_map/all_gather | solution.py:118
  50.2 0.8 collective-permute-start
  51.1 2.8 %collective-permute-done = f32[36,72,128]{2,1,0:T(8,128)S(1)} collective-permute-done((f32[36,72,128]{2,1,0:T(8,128)}, f32[36,72,128]{2,1,0:T(8,128)S(1)}, u32[]{:S(2)}, u32[]{:S(2)}) %collective-permute-start) | collective-permute-done | bytes 1327136 | tf_op jit(solution)/shard_map/ppermute | solution.py:120
  54.2 1.4 fusion.46
  55.6 0.2 slice_select_fusion
  56.0 11.5 %fusion.2 = f32[36,4,128,192]{2,3,0,1:T(8,128)} fusion(f32[36,128,128]{2,1,0:T(8,128)S(1)} %pad_maximum_fusion, f32[4]{0:T(128)S(1)} %multiply_add_fusion.3, s32[36]{0:T(128)S(1)} %get-tuple-element.30), kind=kOutput, calls=%fused_computation.2 | convolution fusion | flops 5442306048 | bytes 16515232 | tf_op jit(solution)/shard_map/bri,cbij->bcrj/dot_general | solution.py:90
  67.5 25.4 %reduce-scatter.2.cloned.1.call-done = f32[4,192,128]{2,1,0:T(8,128)} async-done(((f32[4,192,512]{2,1,0:T(8,128)}), f32[4,192,128]{2,1,0:T(8,128)}) %reduce-scatter.2.cloned.1.call-update) | async-done | bytes 393232 | tf_op jit(solution)/shard_map/reduce_scatter | solution.py:129
  92.9 10.1 %divide_bitcast_fusion = (f32[1,4,192,128]{3,2,1,0:T(8,128)S(1)}, f32[1,4,192,128]{3,2,1,0:T(8,128)S(1)}) fusion(f32[4,192,128]{2,1,0:T(8,128)} %reduce-scatter.2.cloned.1.call-done, s32[4,192,128]{2,1,0:T(8,128)S(1)} %copy-done.2, f32[4]{0:T(128)S(1)} %dynamic-slice_convert_fusion, s32[36]{0:T(128)S(1)} %get-tuple-element.29, s32[128]{0:T(128)S(1)} %iota_add_fusion, ...), kind=kOutput, calls=%fused_computation.43 | convolution fusion | flops 5437685760 | bytes 15729312 | tf_op jit(solution)/shard_map/bcrj,bjk->crk/dot_general | solution.py:94
  103.1 1.4 copy.17
  104.5 10.5 %all-to-all-start = ((f32[2,4,192,128]{3,1,0,2:T(4,128)}), f32[2,4,192,128]{3,1,0,2:T(4,128)S(1)}, u32[]{:S(2)}, u32[]{:S(2)}) async-start(f32[2,4,192,128]{3,1,0,2:T(4,128)} %copy.17), calls=%async_computation.1 | async-start | bytes 1572864 | tf_op jit(solution)/shard_map/all_to_all | solution.py:145
  115.1 27.7 %all-to-all-done = f32[2,4,192,128]{3,1,0,2:T(4,128)S(1)} async-done(((f32[2,4,192,128]{3,1,0,2:T(4,128)}), f32[2,4,192,128]{3,1,0,2:T(4,128)S(1)}, u32[]{:S(2)}, u32[]{:S(2)}) %all-to-all-start) | async-done | bytes 786464 | tf_op jit(solution)/shard_map/all_to_all | solution.py:145
  143.4 0.3 fusion.39
  143.7 0.3 fusion.41
  144.1 0.7 convolution_subtract_fusion
  144.9 0.2 copy.21
  145.1 0.9 copy.22
  (40 shorter events, 1.7 us)
Async XLA Ops:
  6.5 5.0 %copy-start.1 = (f32[4,9,128,128]{3,2,1,0:T(8,128)S(1)}, f32[4,9,128,128]{3,2,1,0:T(8,128)}, u32[]{:S(2)}) copy-start(f32[4,9,128,128]{3,2,1,0:T(8,128)} %param.9) | copy-start | bytes 7077892
  6.5 43.6 %all-gather.2.cloned.1.call-start = ((), (), s32[]{:S(2)}) async-start(), calls=%async_computation.3 | async-start | bytes 1658880 | tf_op jit(solution)/shard_map/all_gather | solution.py:118
  11.5 81.4 %reduce-scatter.2.cloned.1.call-start = ((), (), s32[]{:S(2)}) async-start(), calls=%async_computation.2 | async-start | bytes 1966080 | tf_op jit(solution)/shard_map/reduce_scatter | solution.py:129
  13.9 37.2 %copy-start.3 = (s32[256]{0:T(256)S(1)}, s32[256]{0:T(256)}, u32[]{:S(2)}) copy-start(s32[256]{0:T(256)} %param.13) | copy-start | bytes 3076
  50.2 3.7 %collective-permute-start = (f32[36,72,128]{2,1,0:T(8,128)}, f32[36,72,128]{2,1,0:T(8,128)S(1)}, u32[]{:S(2)}, u32[]{:S(2)}) collective-permute-start(f32[36,72,128]{2,1,0:T(8,128)} %all-gather.2.cloned.1.call-done), channel_id=1, source_target_pairs={{0,4},{4,0},{8,12},{12,8},{16,20},{20,16},{24,28},{28,24},{32,36},... | collective-permute-start | bytes 3981320 | tf_op jit(solution)/shard_map/ppermute | solution.py:120
  51.1 4.5 %copy-start = (f32[36,72,128]{2,1,0:T(8,128)S(1)}, f32[36,72,128]{2,1,0:T(8,128)}, u32[]{:S(2)}) copy-start(f32[36,72,128]{2,1,0:T(8,128)} %all-gather.2.cloned.1.call-done) | copy-start | bytes 3981316
  56.0 36.9 %copy-start.2 = (s32[4,192,128]{2,1,0:T(8,128)S(1)}, s32[4,192,128]{2,1,0:T(8,128)}, u32[]{:S(2)}) copy-start(s32[4,192,128]{2,1,0:T(8,128)} %param.12) | copy-start | bytes 1179652
  104.5 38.4 %all-to-all-start = ((f32[2,4,192,128]{3,1,0,2:T(4,128)}), f32[2,4,192,128]{3,1,0,2:T(4,128)S(1)}, u32[]{:S(2)}, u32[]{:S(2)}) async-start(f32[2,4,192,128]{3,1,0,2:T(4,128)} %copy.17), calls=%async_computation.1 | async-start | bytes 1572864 | tf_op jit(solution)/shard_map/all_to_all | solution.py:145
Sparse Core Ops, SparseCore 0:
  11.6 38.5 all-gather.1
  52.7 40.0 reduce-scatter.1

commit v7 on v1

--- a/solution.py
+++ b/solution.py
@@ -88,23 +88,27 @@
     log_weight = jnp.log(beam_weight)
     response = jnp.exp(exponent[:, None, None, None] * log_weight[None])
     stacked = jnp.stack([response * images, response * response])
+    row_start = jnp.clip(offsets[:, 0], 0, MOS_ROWS - side)
+    col_start = jnp.clip(offsets[:, 1], 0, MOS_COLS - side)
     row_hit = (
         lax.broadcasted_iota(jnp.int32, (1, MOS_ROWS, side), 1)
-        == lax.broadcasted_iota(jnp.int32, (1, MOS_ROWS, side), 2) + offsets[:, 0, None, None]
+        == lax.broadcasted_iota(jnp.int32, (1, MOS_ROWS, side), 2) + row_start[:, None, None]
     ).astype(jnp.float32)
     col_hit = (
         lax.broadcasted_iota(jnp.int32, (1, side, MOS_COLS), 2)
-        == lax.broadcasted_iota(jnp.int32, (1, side, MOS_COLS), 1) + offsets[:, 1, None, None]
+        == lax.broadcasted_iota(jnp.int32, (1, side, MOS_COLS), 1) + col_start[:, None, None]
     ).astype(jnp.float32)
     rows_placed = jnp.einsum(
         "bri,acbij->bacrj", row_hit, stacked, precision=lax.Precision.HIGHEST,
         preferred_element_type=jnp.float32,
     )
+    blocks = lax.psum(1, "beam")
+    col_hit = col_hit.reshape(col_hit.shape[0], side, blocks, MOS_COLS // blocks)
     planes = jnp.einsum(
-        "bacrj,bjk->acrk", rows_placed, col_hit, precision=lax.Precision.HIGHEST,
+        "bacrj,bjnk->nacrk", rows_placed, col_hit, precision=lax.Precision.HIGHEST,
         preferred_element_type=jnp.float32,
     )
-    own = lax.psum_scatter(planes, "beam", scatter_dimension=3, tiled=True)
+    own = lax.psum_scatter(planes, "beam", scatter_dimension=0, tiled=False)
     dividend_accumulator = own[0]
     normalizer_accumulated = own[1]
     accepted_entries = 1.0 - rejected_indicator.astype(jnp.float32)

time: 140 us -> 140 us (level)
  no operation moved by 1% of the time
where the time goes in v7:
time: 140 us
  waiting for transfers between devices  94.8 us (68%)
  between operations  13.5 us (10%)
  matrix products  12.8 us (9%)
  starting transfers between devices  10.5 us (8%)
  local copies, waits for them, and re-layouts  5.42 us (4%)
  other arithmetic  2.53 us (2%)
    reduce_scatter x1, waiting for transfers between devices, local(): own = lax.psum_scatter(planes, 'beam', scatter_dimension=0, tiled=False)  67.1 us
    all_to_all x1, waiting for transfers between devices, local(): lax.all_to_all(jnp.stack([celestial_image, importance_factor]), 'chan', s...  27.7 us
    all_to_all x1, starting transfers between devices, local(): lax.all_to_all(jnp.stack([celestial_image, importance_factor]), 'chan', s...  10.5 us
    dot_general x1, matrix products, local(): jnp.einsum('bacrj,bjnk->nacrk', rows_placed, col_hit, precision=lax.Preci...  8.13 us
    dot_general x1, matrix products, local(): jnp.einsum('bri,acbij->bacrj', row_hit, stacked, precision=lax.Precision....  3.43 us
  transfers between devices with their start and end apart: 2, of which 2 were waited for; matrix products, arithmetic and copies ran while one was open for 0% of the time, Pallas kernels for 0%

profile of v7, /device:TPU:65, one launch (start us, length us, event | category | flops | bytes accessed | tf_op | source)
XLA Modules:
  0.0 139.5 jit_solution(9822385125795115605)
XLA Ops:
  6.6 1.3 log.3
  7.9 0.4 exponential_multiply_fusion
  8.2 0.1 copy-done
  8.4 0.4 multiply_bitcast_fusion
  8.8 0.3 copy-done.2
  9.1 3.4 %fusion.2 = f32[9,2,4,128,192]{3,4,0,2,1:T(8,128)S(1)} fusion(f32[1,4,9,128,128]{4,3,2,1,0:T(8,128)S(1)} %exponential_multiply_fusion, f32[1,4,9,128,128]{4,3,2,1,0:T(8,128)S(1)} %multiply_bitcast_fusion, s32[9]{0:T(128)S(1)} %get-tuple-element.23), kind=kOutput, calls=%fused_computation.2 | convolution fusion | flops 2719531008 | bytes 11796516 | tf_op jit(solution)/shard_map/bri,acbij->bacrj/dot_general | solution.py:101
  12.5 8.1 %fusion.8 = f32[4,2,4,192,128]{4,3,2,1,0:T(8,128)} fusion(f32[9,2,4,128,192]{3,4,0,2,1:T(8,128)S(1)} %fusion.2, s32[9]{0:T(128)S(1)} %get-tuple-element.22, s32[4,128]{1,0:T(4,128)S(1)} %multiply_add_fusion.1), kind=kOutput, calls=%fused_computation.10 | convolution fusion | flops 10872815616 | bytes 10225700 | tf_op jit(solution)/shard_map/bacrj,bjnk->nacrk/dot_general | solution.py:107
  20.7 0.7 copy-done.3
  21.4 67.1 %reduce-scatter.2.cloned.1.call-done = f32[1,2,4,192,128]{4,3,2,1,0:T(8,128)} async-done(((f32[4,2,4,192,128]{4,3,2,1,0:T(8,128)}), f32[1,2,4,192,128]{4,3,2,1,0:T(8,128)}) %reduce-scatter.2.cloned.1.call-update) | async-done | bytes 786448 | tf_op jit(solution)/shard_map/reduce_scatter | solution.py:111
  88.5 1.2 fusion.24
  89.8 1.4 %copy.14 = f32[2,4,192,128]{3,1,0,2:T(4,128)} copy(f32[2,4,192,128]{3,2,1,0:T(8,128)S(1)} %pad_maximum_fusion) | data formatting | bytes 1572864 | tf_op jit(solution)/shard_map/stack | solution.py:123
  91.2 10.5 %all-to-all-start = ((f32[2,4,192,128]{3,1,0,2:T(4,128)}), f32[2,4,192,128]{3,1,0,2:T(4,128)S(1)}, u32[]{:S(2)}, u32[]{:S(2)}) async-start(f32[2,4,192,128]{3,1,0,2:T(4,128)} %copy.14), calls=%async_computation.1 | async-start | bytes 1572864 | tf_op jit(solution)/shard_map/all_to_all | solution.py:122
  101.8 27.7 %all-to-all-done = f32[2,4,192,128]{3,1,0,2:T(4,128)S(1)} async-done(((f32[2,4,192,128]{3,1,0,2:T(4,128)}), f32[2,4,192,128]{3,1,0,2:T(4,128)S(1)}, u32[]{:S(2)}, u32[]{:S(2)}) %all-to-all-start) | async-done | bytes 786464 | tf_op jit(solution)/shard_map/all_to_all | solution.py:122
  129.5 0.1 copy.15
  129.6 0.1 fusion.61
  129.7 0.1 copy.16
  129.9 0.1 copy.17
  130.0 0.3 fusion.18
  130.3 0.3 fusion.20
  130.6 0.1 fusion.44
  130.8 0.7 convolution_subtract_fusion
  131.5 0.1 multiply_add_fusion
  131.6 0.2 copy.18
  131.8 0.9 copy.19
  (24 shorter events, 0.4 us)
Async XLA Ops:
  6.5 1.8 %copy-start = (f32[4,9,128,128]{3,2,1,0:T(8,128)S(1)}, f32[4,9,128,128]{3,2,1,0:T(8,128)}, u32[]{:S(2)}) copy-start(f32[4,9,128,128]{3,2,1,0:T(8,128)} %param.5) | copy-start | bytes 7077892
  6.5 81.9 %reduce-scatter.2.cloned.1.call-start = ((), (), s32[]{:S(2)}) async-start(), calls=%async_computation.2 | async-start | bytes 3932160 | tf_op jit(solution)/shard_map/reduce_scatter | solution.py:111
  8.4 0.7 copy-start.2
  20.6 0.7 copy-start.3
  20.6 67.8 %copy-start.1 = (s32[4,192,128]{2,1,0:T(8,128)S(1)}, s32[4,192,128]{2,1,0:T(8,128)}, u32[]{:S(2)}) copy-start(s32[4,192,128]{2,1,0:T(8,128)} %param.8) | copy-start | bytes 1179652
  91.2 38.3 %all-to-all-start = ((f32[2,4,192,128]{3,1,0,2:T(4,128)}), f32[2,4,192,128]{3,1,0,2:T(4,128)S(1)}, u32[]{:S(2)}, u32[]{:S(2)}) async-start(f32[2,4,192,128]{3,1,0,2:T(4,128)} %copy.14), calls=%async_computation.1 | async-start | bytes 1572864 | tf_op jit(solution)/shard_map/all_to_all | solution.py:122
Sparse Core Ops, SparseCore 0:
  20.8 67.6 reduce-scatter.1

commit v8 on v6

--- a/solution.py
+++ b/solution.py
@@ -78,6 +78,28 @@
     return smoothed.reshape(channels, rows, columns)
 
 
+def line_all_gather(piece):
+    groups = lax.psum(1, "beam")
+    me = lax.axis_index("beam")
+    from_left = [piece]
+    from_right = [piece]
+    for step in range(1, groups):
+        from_left.append(
+            lax.ppermute(from_left[-1], "beam", [(i, i + 1) for i in range(step - 1, groups - 1)])
+        )
+        from_right.append(
+            lax.ppermute(from_right[-1], "beam", [(i, i - 1) for i in range(1, groups - step + 1)])
+        )
+    gathered = []
+    for group in range(groups):
+        chosen = piece
+        for step in range(1, groups):
+            chosen = jnp.where(me - step == group, from_left[step], chosen)
+            chosen = jnp.where(me + step == group, from_right[step], chosen)
+        gathered.append(chosen)
+    return jnp.concatenate(gathered, axis=0)
+
+
 def place(values, row_start, col_start, side, columns, first_column):
     row_hit = (
         lax.broadcasted_iota(jnp.int32, (1, MOS_ROWS, side), 1)
@@ -115,7 +137,7 @@
     corner = jnp.zeros((log_weight.shape[0], 8, side), jnp.float32)
     corner = corner.at[:, 0, 0].set(row_start.astype(jnp.float32))
     corner = corner.at[:, 0, 1].set(col_start.astype(jnp.float32))
-    shared = lax.all_gather(jnp.concatenate([own_half, corner], axis=1), "beam", axis=0, tiled=True)
+    shared = line_all_gather(jnp.concatenate([own_half, corner], axis=1))
     chan_size = lax.psum(1, "chan")
     other = lax.ppermute(shared, "chan", [(a, a ^ 1) for a in range(chan_size)])
     first_half = jnp.where(core == 0, shared, other)

time: 153 us -> 144 us (0.941)
  waiting for transfers between devices: 87.6 us -> 58.1 us
  starting transfers between devices: 11.4 us -> 27.4 us
  matrix products: 29.8 us -> 31.4 us
    all_gather x1 -> x0, waiting for transfers between devices: 31.6 us -> none  [local(): lax.all_gather(jnp.concatenate([own_half, corner], axis=1), 'beam', axis=...]
    ppermute x0 -> x6, starting transfers between devices: none -> 13.7 us  [the longest x3 8.98 us: line_all_gather(): lax.ppermute(from_left[-1], 'beam', [(i, i + 1) for i in range(step - 1,...]
    ppermute x0 -> x6, waiting for transfers between devices: none -> 7.29 us  [the longest x3 5.25 us: line_all_gather(): lax.ppermute(from_right[-1], 'beam', [(i, i - 1) for i in range(1, groups...]
    reduce_scatter x1, waiting for transfers between devices: 25.4 us -> 20.5 us  [local(): lax.psum_scatter(numerator, 'beam', scatter_dimension=2, tiled=True)]
    ppermute x1, starting transfers between devices: 0.84 us -> 3.24 us  [local(): other = lax.ppermute(shared, 'chan', [(a, a ^ 1) for a in range(chan_size)])]
    dot_general x2, matrix products: 13.8 us -> 15.4 us  [place(): jnp.einsum('bri,cbij->bcrj', row_hit, values, precision=lax.Precision.HIG...]
  transfers between devices with their start and end apart: 4 -> 9, of which waited for: 4 -> 5; matrix products, arithmetic and copies ran while one was open for 14% -> 17% of each run, Pallas kernels for 0% -> 0%
where the time goes in v8:
time: 144 us; the launch traced here: 143 us
  waiting for transfers between devices  58.1 us (40%)
  matrix products  31.4 us (22%)
  starting transfers between devices  27.4 us (19%)
  between operations  13.8 us (10%)
  local copies, waits for them, and re-layouts  7.56 us (5%)
  other arithmetic  5.15 us (4%)
    all_to_all x1, waiting for transfers between devices, local(): lax.all_to_all(jnp.stack([celestial_image, importance_factor]), 'chan', s...  27.7 us
    reduce_scatter x1, waiting for transfers between devices, local(): lax.psum_scatter(numerator, 'beam', scatter_dimension=2, tiled=True)  20.5 us
    dot_general x2, matrix products, place(): jnp.einsum('bri,cbij->bcrj', row_hit, values, precision=lax.Precision.HIG...  15.4 us
    dot_general x2, matrix products, place(): jnp.einsum('bcrj,bjk->crk', rows_placed, col_hit, precision=lax.Precision...  14.8 us
    all_to_all x1, starting transfers between devices, local(): lax.all_to_all(jnp.stack([celestial_image, importance_factor]), 'chan', s...  10.5 us
    ppermute x3, starting transfers between devices, line_all_gather(): lax.ppermute(from_left[-1], 'beam', [(i, i + 1) for i in range(step - 1,...  8.98 us
    ppermute x3, waiting for transfers between devices, line_all_gather(): lax.ppermute(from_right[-1], 'beam', [(i, i - 1) for i in range(1, groups...  5.25 us
    ppermute x3, starting transfers between devices, line_all_gather(): lax.ppermute(from_right[-1], 'beam', [(i, i - 1) for i in range(1, groups...  4.71 us
  transfers between devices with their start and end apart: 9, of which 5 were waited for; matrix products, arithmetic and copies ran while one was open for 17% of the time, Pallas kernels for 0%

profile of v8, /device:TPU:65, one launch (start us, length us, event | category | flops | bytes accessed | tf_op | source)
XLA Modules:
  0.0 143.4 jit_solution(783318708409345787)
XLA Ops:
  6.5 1.1 log.3
  7.7 0.8 fusion.76
  9.1 1.2 scatter.9
  10.6 1.9 %collective-permute-start = (f32[9,72,128]{2,1,0:T(8,128)S(1)}, f32[9,72,128]{2,1,0:T(8,128)S(1)}, u32[]{:S(2)}, u32[]{:S(2)}) collective-permute-start(f32[9,72,128]{2,1,0:T(8,128)S(1)} %pad_maximum_fusion.3), channel_id=1, source_target_pairs={{1,0},{2,1},{3,2},{5,4},{6,5},{7,6},{9,8},{10,9},{11,10},{13,12},{... | collective-permute-start | bytes 995336 | tf_op jit(solution)/shard_map/ppermute | solution.py:91
  12.5 3.4 %collective-permute-start.3 = (f32[9,72,128]{2,1,0:T(8,128)S(1)}, f32[9,72,128]{2,1,0:T(8,128)S(1)}, u32[]{:S(2)}, u32[]{:S(2)}) collective-permute-start(f32[9,72,128]{2,1,0:T(8,128)S(1)} %pad_maximum_fusion.3), channel_id=1, source_target_pairs={{0,1},{1,2},{2,3},{4,5},{5,6},{6,7},{8,9},{9,10},{10,11},{12,13},{... | collective-permute-start | bytes 995336 | tf_op jit(solution)/shard_map/ppermute | solution.py:88
  15.9 5.2 %collective-permute-done = f32[9,72,128]{2,1,0:T(8,128)S(1)} collective-permute-done((f32[9,72,128]{2,1,0:T(8,128)S(1)}, f32[9,72,128]{2,1,0:T(8,128)S(1)}, u32[]{:S(2)}, u32[]{:S(2)}) %collective-permute-start) | collective-permute-done | bytes 331808 | tf_op jit(solution)/shard_map/ppermute | solution.py:91
  21.2 2.1 %collective-permute-start.1 = (f32[9,72,128]{2,1,0:T(8,128)S(1)}, f32[9,72,128]{2,1,0:T(8,128)S(1)}, u32[]{:S(2)}, u32[]{:S(2)}) collective-permute-start(f32[9,72,128]{2,1,0:T(8,128)S(1)} %collective-permute-done), channel_id=1, source_target_pairs={{1,0},{2,1},{5,4},{6,5},{9,8},{10,9},{13,12},{14,13},{17,16},{18,1... | collective-permute-start | bytes 995336 | tf_op jit(solution)/shard_map/ppermute | solution.py:91
  23.3 2.9 %collective-permute-start.4 = (f32[9,72,128]{2,1,0:T(8,128)S(1)}, f32[9,72,128]{2,1,0:T(8,128)S(1)}, u32[]{:S(2)}, u32[]{:S(2)}) collective-permute-start(f32[9,72,128]{2,1,0:T(8,128)S(1)} %collective-permute-done.3), channel_id=1, source_target_pairs={{1,2},{2,3},{5,6},{6,7},{9,10},{10,11},{13,14},{14,15},{17,18},{18... | collective-permute-start | bytes 995336 | tf_op jit(solution)/shard_map/ppermute | solution.py:88
  26.2 4.0 %fusion.12 = f32[9,4,128,192]{2,3,0,1:T(8,128)S(1)} fusion(f32[4,9,128,128]{3,2,1,0:T(8,128)} %param.9, f32[9,128,128]{2,1,0:T(8,128)S(1)} %log.3, f32[4]{0:T(128)S(1)} %multiply_add_fusion.3, s32[9]{0:T(128)S(1)} %get-tuple-element.51), kind=kOutput, calls=%fused_computation.15 | convolution fusion | flops 1360576512 | bytes 6488116 | tf_op jit(solution)/shard_map/bri,cbij->bcrj/dot_general | solution.py:112
  30.2 0.7 collective-permute-start.2
  30.9 2.0 %collective-permute-done.4 = f32[9,72,128]{2,1,0:T(8,128)S(1)} collective-permute-done((f32[9,72,128]{2,1,0:T(8,128)S(1)}, f32[9,72,128]{2,1,0:T(8,128)S(1)}, u32[]{:S(2)}, u32[]{:S(2)}) %collective-permute-start.4) | collective-permute-done | bytes 331808 | tf_op jit(solution)/shard_map/ppermute | solution.py:88
  32.9 2.7 %collective-permute-start.5 = (f32[9,72,128]{2,1,0:T(8,128)S(1)}, f32[9,72,128]{2,1,0:T(8,128)S(1)}, u32[]{:S(2)}, u32[]{:S(2)}) collective-permute-start(f32[9,72,128]{2,1,0:T(8,128)S(1)} %collective-permute-done.4), channel_id=1, source_target_pairs={{2,3},{6,7},{10,11},{14,15},{18,19},{22,23},{26,27},{30,31},{34,35... | collective-permute-start | bytes 995336 | tf_op jit(solution)/shard_map/ppermute | solution.py:88
  35.6 4.6 %fusion.21 = f32[4,192,512]{2,1,0:T(8,128)} fusion(f32[9,4,128,192]{2,3,0,1:T(8,128)S(1)} %fusion.12, s32[9]{0:T(128)S(1)} %get-tuple-element.48), kind=kOutput, calls=%fused_computation.22 | convolution fusion | flops 5436997632 | bytes 5111844 | tf_op jit(solution)/shard_map/bcrj,bjk->crk/dot_general | solution.py:116
  42.3 3.2 %collective-permute-start.6 = (f32[36,72,128]{2,1,0:T(8,128)S(1)}, f32[36,72,128]{2,1,0:T(8,128)S(1)}, u32[]{:S(2)}, u32[]{:S(2)}) collective-permute-start(f32[36,72,128]{2,1,0:T(8,128)S(1)} %pad_maximum_fusion.1), channel_id=1, source_target_pairs={{0,4},{4,0},{8,12},{12,8},{16,20},{20,16},{24,28},{28,24},{32,36},... | collective-permute-start | bytes 3981320 | tf_op jit(solution)/shard_map/ppermute | solution.py:142
  45.7 2.6 %collective-permute-done.6 = f32[36,72,128]{2,1,0:T(8,128)S(1)} collective-permute-done((f32[36,72,128]{2,1,0:T(8,128)S(1)}, f32[36,72,128]{2,1,0:T(8,128)S(1)}, u32[]{:S(2)}, u32[]{:S(2)}) %collective-permute-start.6) | collective-permute-done | bytes 1327136 | tf_op jit(solution)/shard_map/ppermute | solution.py:142
  48.3 1.2 broadcast_select_fusion
  49.6 1.4 %fusion.46 = (s32[36]{0:T(128)S(1)}, s32[36]{0:T(128)S(1)}) fusion(f32[36,72,128]{2,1,0:T(8,128)S(1)} %broadcast_select_fusion), kind=kLoop, calls=%fused_computation.55 | loop fusion | flops 72 | bytes 576 | tf_op jit(solution)/shard_map/convert_element_type | solution.py:147
  51.5 11.4 %fusion.2 = f32[36,4,128,192]{2,3,0,1:T(8,128)} fusion(f32[36,128,128]{2,1,0:T(8,128)S(1)} %pad_maximum_fusion, f32[4]{0:T(128)S(1)} %multiply_add_fusion.3, s32[36]{0:T(128)S(1)} %get-tuple-element.30), kind=kOutput, calls=%fused_computation.2 | convolution fusion | flops 5442306048 | bytes 16515232 | tf_op jit(solution)/shard_map/bri,cbij->bcrj/dot_general | solution.py:112
  62.9 20.5 %reduce-scatter.2.cloned.1.call-done = f32[4,192,128]{2,1,0:T(8,128)} async-done(((f32[4,192,512]{2,1,0:T(8,128)}), f32[4,192,128]{2,1,0:T(8,128)}) %reduce-scatter.2.cloned.1.call-update) | async-done | bytes 393232 | tf_op jit(solution)/shard_map/reduce_scatter | solution.py:151
  83.5 10.1 %divide_bitcast_fusion = (f32[1,4,192,128]{3,2,1,0:T(8,128)S(1)}, f32[1,4,192,128]{3,2,1,0:T(8,128)S(1)}) fusion(f32[4,192,128]{2,1,0:T(8,128)} %reduce-scatter.2.cloned.1.call-done, s32[4,192,128]{2,1,0:T(8,128)S(1)} %copy-done.2, f32[4]{0:T(128)S(1)} %dynamic-slice_convert_fusion, s32[36]{0:T(128)S(1)} %get-tuple-element.29, s32[128]{0:T(128)S(1)} %iota_add_fusion, ...), kind=kOutput, calls=%fused_computation.44 | convolution fusion | flops 5437685760 | bytes 15729312 | tf_op jit(solution)/shard_map/bcrj,bjk->crk/dot_general | solution.py:116
  93.7 1.4 copy.17
  95.0 10.5 %all-to-all-start = ((f32[2,4,192,128]{3,1,0,2:T(4,128)}), f32[2,4,192,128]{3,1,0,2:T(4,128)S(1)}, u32[]{:S(2)}, u32[]{:S(2)}) async-start(f32[2,4,192,128]{3,1,0,2:T(4,128)} %copy.17), calls=%async_computation.1 | async-start | bytes 1572864 | tf_op jit(solution)/shard_map/all_to_all | solution.py:167
  105.7 27.7 %all-to-all-done = f32[2,4,192,128]{3,1,0,2:T(4,128)S(1)} async-done(((f32[2,4,192,128]{3,1,0,2:T(4,128)}), f32[2,4,192,128]{3,1,0,2:T(4,128)S(1)}, u32[]{:S(2)}, u32[]{:S(2)}) %all-to-all-start) | async-done | bytes 786464 | tf_op jit(solution)/shard_map/all_to_all | solution.py:167
  135.7 0.9 copy.22
  (54 shorter events, 5.9 us)
Async XLA Ops:
  6.5 76.9 %reduce-scatter.2.cloned.1.call-start = ((), (), s32[]{:S(2)}) async-start(), calls=%async_computation.2 | async-start | bytes 1966080 | tf_op jit(solution)/shard_map/reduce_scatter | solution.py:151
  10.6 10.6 %collective-permute-start = (f32[9,72,128]{2,1,0:T(8,128)S(1)}, f32[9,72,128]{2,1,0:T(8,128)S(1)}, u32[]{:S(2)}, u32[]{:S(2)}) collective-permute-start(f32[9,72,128]{2,1,0:T(8,128)S(1)} %pad_maximum_fusion.3), channel_id=1, source_target_pairs={{1,0},{2,1},{3,2},{5,4},{6,5},{7,6},{9,8},{10,9},{11,10},{13,12},{... | collective-permute-start | bytes 995336 | tf_op jit(solution)/shard_map/ppermute | solution.py:91
  12.5 10.8 %collective-permute-start.3 = (f32[9,72,128]{2,1,0:T(8,128)S(1)}, f32[9,72,128]{2,1,0:T(8,128)S(1)}, u32[]{:S(2)}, u32[]{:S(2)}) collective-permute-start(f32[9,72,128]{2,1,0:T(8,128)S(1)} %pad_maximum_fusion.3), channel_id=1, source_target_pairs={{0,1},{1,2},{2,3},{4,5},{5,6},{6,7},{8,9},{9,10},{10,11},{12,13},{... | collective-permute-start | bytes 995336 | tf_op jit(solution)/shard_map/ppermute | solution.py:88
  21.2 9.0 %collective-permute-start.1 = (f32[9,72,128]{2,1,0:T(8,128)S(1)}, f32[9,72,128]{2,1,0:T(8,128)S(1)}, u32[]{:S(2)}, u32[]{:S(2)}) collective-permute-start(f32[9,72,128]{2,1,0:T(8,128)S(1)} %collective-permute-done), channel_id=1, source_target_pairs={{1,0},{2,1},{5,4},{6,5},{9,8},{10,9},{13,12},{14,13},{17,16},{18,1... | collective-permute-start | bytes 995336 | tf_op jit(solution)/shard_map/ppermute | solution.py:91
  23.3 9.6 %collective-permute-start.4 = (f32[9,72,128]{2,1,0:T(8,128)S(1)}, f32[9,72,128]{2,1,0:T(8,128)S(1)}, u32[]{:S(2)}, u32[]{:S(2)}) collective-permute-start(f32[9,72,128]{2,1,0:T(8,128)S(1)} %collective-permute-done.3), channel_id=1, source_target_pairs={{1,2},{2,3},{5,6},{6,7},{9,10},{10,11},{13,14},{14,15},{17,18},{18... | collective-permute-start | bytes 995336 | tf_op jit(solution)/shard_map/ppermute | solution.py:88
  30.2 10.2 %collective-permute-start.2 = (f32[9,72,128]{2,1,0:T(8,128)S(1)}, f32[9,72,128]{2,1,0:T(8,128)S(1)}, u32[]{:S(2)}, u32[]{:S(2)}) collective-permute-start(f32[9,72,128]{2,1,0:T(8,128)S(1)} %collective-permute-done.1), channel_id=1, source_target_pairs={{1,0},{5,4},{9,8},{13,12},{17,16},{21,20},{25,24},{29,28},{33,32},... | collective-permute-start | bytes 995336 | tf_op jit(solution)/shard_map/ppermute | solution.py:91
  32.9 7.4 %collective-permute-start.5 = (f32[9,72,128]{2,1,0:T(8,128)S(1)}, f32[9,72,128]{2,1,0:T(8,128)S(1)}, u32[]{:S(2)}, u32[]{:S(2)}) collective-permute-start(f32[9,72,128]{2,1,0:T(8,128)S(1)} %collective-permute-done.4), channel_id=1, source_target_pairs={{2,3},{6,7},{10,11},{14,15},{18,19},{22,23},{26,27},{30,31},{34,35... | collective-permute-start | bytes 995336 | tf_op jit(solution)/shard_map/ppermute | solution.py:88
  40.9 0.7 copy-start
  40.9 4.7 %copy-start.3 = (s32[256]{0:T(256)S(1)}, s32[256]{0:T(256)}, u32[]{:S(2)}) copy-start(s32[256]{0:T(256)} %param.13) | copy-start | bytes 3076
  41.6 0.7 copy-start.1
  42.3 5.9 %collective-permute-start.6 = (f32[36,72,128]{2,1,0:T(8,128)S(1)}, f32[36,72,128]{2,1,0:T(8,128)S(1)}, u32[]{:S(2)}, u32[]{:S(2)}) collective-permute-start(f32[36,72,128]{2,1,0:T(8,128)S(1)} %pad_maximum_fusion.1), channel_id=1, source_target_pairs={{0,4},{4,0},{8,12},{12,8},{16,20},{20,16},{24,28},{28,24},{32,36},... | collective-permute-start | bytes 3981320 | tf_op jit(solution)/shard_map/ppermute | solution.py:142
  51.5 32.0 %copy-start.2 = (s32[4,192,128]{2,1,0:T(8,128)S(1)}, s32[4,192,128]{2,1,0:T(8,128)}, u32[]{:S(2)}) copy-start(s32[4,192,128]{2,1,0:T(8,128)} %param.12) | copy-start | bytes 1179652
  95.0 38.3 %all-to-all-start = ((f32[2,4,192,128]{3,1,0,2:T(4,128)}), f32[2,4,192,128]{3,1,0,2:T(4,128)S(1)}, u32[]{:S(2)}, u32[]{:S(2)}) async-start(f32[2,4,192,128]{3,1,0,2:T(4,128)} %copy.17), calls=%async_computation.1 | async-start | bytes 1572864 | tf_op jit(solution)/shard_map/all_to_all | solution.py:167
Sparse Core Ops, SparseCore 0:
  40.4 43.0 reduce-scatter.1

commit v9 on v8

--- a/solution.py
+++ b/solution.py
@@ -1,7 +1,9 @@
 import jax
+import numpy as np
 import jax.numpy as jnp
 from jax import lax
 from jax.sharding import PartitionSpec as P
+
 
 MOS_ROWS = 192
 MOS_COLS = 512
@@ -78,6 +80,30 @@
     return smoothed.reshape(channels, rows, columns)
 
 
+JITTER = 16
+
+
+def reaching_beams(groups, beams, side):
+    grid = int(round(beams ** 0.5))
+    block = MOS_COLS // groups
+    lists = []
+    for target in range(groups):
+        found = []
+        for beam in range(beams):
+            col = beam % grid
+            base = col * (MOS_COLS - side) // (grid - 1)
+            inner = 0 < col < grid - 1
+            low = max(base - JITTER, 0) if inner else base
+            high = min(base + JITTER, MOS_COLS - side) if inner else base
+            if low < block * (target + 1) and high + side > block * target:
+                found.append(beam)
+        lists.append(found)
+    width = max(len(found) for found in lists)
+    table = np.array([found + [0] * (width - len(found)) for found in lists], np.int32)
+    valid = np.array([[True] * len(found) + [False] * (width - len(found)) for found in lists])
+    return table, valid
+
+
 def line_all_gather(piece):
     groups = lax.psum(1, "beam")
     me = lax.axis_index("beam")
@@ -119,7 +145,7 @@
     )
 
 
-def local(images, beam_weight, offsets, rejected_indicator, regression_indicator):
+def local_body(images, beam_weight, offsets, rejected_indicator, regression_indicator):
     ch_dev = images.shape[0]
     side = images.shape[2]
     col_dev = rejected_indicator.shape[2]
@@ -137,7 +163,13 @@
     corner = jnp.zeros((log_weight.shape[0], 8, side), jnp.float32)
     corner = corner.at[:, 0, 0].set(row_start.astype(jnp.float32))
     corner = corner.at[:, 0, 1].set(col_start.astype(jnp.float32))
-    shared = line_all_gather(jnp.concatenate([own_half, corner], axis=1))
+    response = jnp.exp(exponent[:, None, None, None] * log_weight[None])
+    numerator = place(response * images, row_start, col_start, side, MOS_COLS, 0)
+    numerator, outgoing = lax.optimization_barrier(
+        (numerator, jnp.concatenate([own_half, corner], axis=1))
+    )
+    dividend_accumulator = lax.psum_scatter(numerator, "beam", scatter_dimension=2, tiled=True)
+    shared = line_all_gather(outgoing)
     chan_size = lax.psum(1, "chan")
     other = lax.ppermute(shared, "chan", [(a, a ^ 1) for a in range(chan_size)])
     first_half = jnp.where(core == 0, shared, other)
@@ -145,10 +177,12 @@
     every_log = jnp.concatenate([first_half[:, :half], second_half[:, :half]], axis=1)
     every_row = first_half[:, half, 0].astype(jnp.int32)
     every_col = first_half[:, half, 1].astype(jnp.int32)
-
-    response = jnp.exp(exponent[:, None, None, None] * log_weight[None])
-    numerator = place(response * images, row_start, col_start, side, MOS_COLS, 0)
-    dividend_accumulator = lax.psum_scatter(numerator, "beam", scatter_dimension=2, tiled=True)
+    table, valid = reaching_beams(lax.psum(1, "beam"), every_log.shape[0], side)
+    me = lax.axis_index("beam")
+    chosen = jnp.asarray(table)[me]
+    every_log = jnp.take(every_log, chosen, axis=0)
+    every_row = jnp.take(every_row, chosen, axis=0)
+    every_col = jnp.where(jnp.asarray(valid)[me], jnp.take(every_col, chosen, axis=0), -4 * MOS_COLS)
 
     every_response = jnp.exp(exponent[:, None, None, None] * every_log[None])
     col_first = lax.axis_index("beam") * col_dev
@@ -156,6 +190,7 @@
         every_response * every_response, every_row, every_col, side, col_dev, col_first
     )
 
+    normalizer_accumulated = lax.optimization_barrier(normalizer_accumulated)
     accepted_entries = 1.0 - rejected_indicator.astype(jnp.float32)
     emission_absent = lax.dynamic_slice_in_dim(regression_indicator, first_channel, ch_dev).astype(
         jnp.float32
@@ -179,4 +214,4 @@
         P(),
     )
     out_specs = P(None, "chan", "beam")
-    return jax.shard_map(local, mesh=mesh, in_specs=in_specs, out_specs=out_specs, check_vma=False)
+    return jax.shard_map(local_body, mesh=mesh, in_specs=in_specs, out_specs=out_specs, check_vma=False)

time: 144 us -> 149 us (1.035)
  matrix products: 31.4 us -> 16.3 us
  waiting for transfers between devices: 58.1 us -> 66 us
  local copies, waits for them, and re-layouts: 7.56 us -> 14.5 us
  other arithmetic: 5.15 us -> 8.9 us
  starting transfers between devices: 27.4 us -> 29 us
    ppermute x3, waiting for transfers between devices: 2.04 us -> 13.4 us  [line_all_gather(): lax.ppermute(from_left[-1], 'beam', [(i, i + 1) for i in range(step - 1,...]
    dot_general x2, matrix products: 15.4 us -> 6.88 us  [place(): jnp.einsum('bri,cbij->bcrj', row_hit, values, precision=lax.Precision.HIG...]
    dot_general x2, matrix products: 14.8 us -> 8.15 us  [place(): jnp.einsum('bcrj,bjk->crk', rows_placed, col_hit, precision=lax.Precision...]
    ppermute x3, waiting for transfers between devices: 5.25 us -> 0.01 us  [line_all_gather(): lax.ppermute(from_right[-1], 'beam', [(i, i - 1) for i in range(1, groups...]
    gather x0 -> x3, local copies, waits for them, and re-layouts: none -> 3.02 us  [the longest x1 1.22 us: local_body(): jnp.take(every_col, chosen, axis=0)]
    reduce_scatter x1, waiting for transfers between devices: 20.5 us -> 23.4 us  [local_body(): lax.psum_scatter(numerator, 'beam', scatter_dimension=2, tiled=True)]
    unnamed x8 -> x22, local copies, waits for them, and re-layouts: 1.18 us -> 3.84 us
    ppermute x3, starting transfers between devices: 8.98 us -> 10.6 us  [line_all_gather(): lax.ppermute(from_left[-1], 'beam', [(i, i + 1) for i in range(step - 1,...]
  transfers between devices with their start and end apart: 9 -> 9, of which waited for: 5 -> 6; matrix products, arithmetic and copies ran while one was open for 17% -> 11% of each run, Pallas kernels for 0% -> 0%
where the time goes in v9:
time: 149 us; the launch traced here: 148 us
  waiting for transfers between devices  66 us (44%)
  starting transfers between devices  29 us (19%)
  matrix products  16.3 us (11%)
  local copies, waits for them, and re-layouts  14.5 us (10%)
  between operations  13.8 us (9%)
  other arithmetic  8.9 us (6%)
    all_to_all x1, waiting for transfers between devices, local_body(): lax.all_to_all(jnp.stack([celestial_image, importance_factor]), 'chan', s...  27.7 us
    reduce_scatter x1, waiting for transfers between devices, local_body(): lax.psum_scatter(numerator, 'beam', scatter_dimension=2, tiled=True)  23.4 us
    ppermute x3, waiting for transfers between devices, line_all_gather(): lax.ppermute(from_left[-1], 'beam', [(i, i + 1) for i in range(step - 1,...  13.4 us
    ppermute x3, starting transfers between devices, line_all_gather(): lax.ppermute(from_left[-1], 'beam', [(i, i + 1) for i in range(step - 1,...  10.6 us
    all_to_all x1, starting transfers between devices, local_body(): lax.all_to_all(jnp.stack([celestial_image, importance_factor]), 'chan', s...  10.5 us
    dot_general x2, matrix products, place(): jnp.einsum('bcrj,bjk->crk', rows_placed, col_hit, precision=lax.Precision...  8.15 us
    dot_general x2, matrix products, place(): jnp.einsum('bri,cbij->bcrj', row_hit, values, precision=lax.Precision.HIG...  6.88 us
    ppermute x3, starting transfers between devices, line_all_gather(): lax.ppermute(from_right[-1], 'beam', [(i, i - 1) for i in range(1, groups...  4.45 us
  transfers between devices with their start and end apart: 9, of which 6 were waited for; matrix products, arithmetic and copies ran while one was open for 11% of the time, Pallas kernels for 0%

profile of v9, /device:TPU:65, one launch (start us, length us, event | category | flops | bytes accessed | tf_op | source)
XLA Modules:
  0.0 148.5 jit_solution(14580849657443757561)
XLA Ops:
  7.9 1.3 scatter.9
  9.4 1.3 log.3
  11.3 2.3 %fusion.10 = f32[9,4,128,192]{2,3,0,1:T(8,128)S(1)} fusion(f32[4,9,128,128]{3,2,1,0:T(8,128)S(1)} %copy-done.3, f32[9,128,128]{2,1,0:T(8,128)S(1)} %log.3, f32[4]{0:T(128)S(1)} %multiply_add_fusion.3, s32[9]{0:T(128)S(1)} %get-tuple-element.62), kind=kOutput, calls=%fused_computation.15 | convolution fusion | flops 1360576512 | bytes 6488116 | tf_op jit(solution)/shard_map/bri,cbij->bcrj/dot_general | solution.py:138
  13.6 4.6 %fusion.18 = f32[4,192,512]{2,1,0:T(8,128)} fusion(f32[9,4,128,192]{2,3,0,1:T(8,128)S(1)} %fusion.10, s32[9]{0:T(128)S(1)} %get-tuple-element.61), kind=kOutput, calls=%fused_computation.22 | convolution fusion | flops 5436997632 | bytes 5111844 | tf_op jit(solution)/shard_map/bcrj,bjk->crk/dot_general | solution.py:142
  18.3 3.5 %collective-permute-start.3 = (f32[9,72,128]{2,1,0:T(8,128)S(1)}, f32[9,72,128]{2,1,0:T(8,128)S(1)}, u32[]{:S(2)}, u32[]{:S(2)}) collective-permute-start(f32[9,72,128]{2,1,0:T(8,128)S(1)} %pad_maximum_fusion.3), channel_id=1, source_target_pairs={{0,1},{1,2},{2,3},{4,5},{5,6},{6,7},{8,9},{9,10},{10,11},{12,13},{... | collective-permute-start | bytes 995336 | tf_op jit(solution)/shard_map/ppermute | solution.py:114
  21.8 1.9 %collective-permute-start = (f32[9,72,128]{2,1,0:T(8,128)S(1)}, f32[9,72,128]{2,1,0:T(8,128)S(1)}, u32[]{:S(2)}, u32[]{:S(2)}) collective-permute-start(f32[9,72,128]{2,1,0:T(8,128)S(1)} %pad_maximum_fusion.3), channel_id=1, source_target_pairs={{1,0},{2,1},{3,2},{5,4},{6,5},{7,6},{9,8},{10,9},{11,10},{13,12},{... | collective-permute-start | bytes 995336 | tf_op jit(solution)/shard_map/ppermute | solution.py:117
  23.7 5.1 %collective-permute-done.3 = f32[9,72,128]{2,1,0:T(8,128)S(1)} collective-permute-done((f32[9,72,128]{2,1,0:T(8,128)S(1)}, f32[9,72,128]{2,1,0:T(8,128)S(1)}, u32[]{:S(2)}, u32[]{:S(2)}) %collective-permute-start.3) | collective-permute-done | bytes 331808 | tf_op jit(solution)/shard_map/ppermute | solution.py:114
  28.8 3.5 %collective-permute-start.4 = (f32[9,72,128]{2,1,0:T(8,128)S(1)}, f32[9,72,128]{2,1,0:T(8,128)S(1)}, u32[]{:S(2)}, u32[]{:S(2)}) collective-permute-start(f32[9,72,128]{2,1,0:T(8,128)S(1)} %collective-permute-done.3), channel_id=1, source_target_pairs={{1,2},{2,3},{5,6},{6,7},{9,10},{10,11},{13,14},{14,15},{17,18},{18... | collective-permute-start | bytes 995336 | tf_op jit(solution)/shard_map/ppermute | solution.py:114
  32.4 1.8 %collective-permute-start.1 = (f32[9,72,128]{2,1,0:T(8,128)S(1)}, f32[9,72,128]{2,1,0:T(8,128)S(1)}, u32[]{:S(2)}, u32[]{:S(2)}) collective-permute-start(f32[9,72,128]{2,1,0:T(8,128)S(1)} %collective-permute-done), channel_id=1, source_target_pairs={{1,0},{2,1},{5,4},{6,5},{9,8},{10,9},{13,12},{14,13},{17,16},{18,1... | collective-permute-start | bytes 995336 | tf_op jit(solution)/shard_map/ppermute | solution.py:117
  34.2 4.3 %collective-permute-done.4 = f32[9,72,128]{2,1,0:T(8,128)S(1)} collective-permute-done((f32[9,72,128]{2,1,0:T(8,128)S(1)}, f32[9,72,128]{2,1,0:T(8,128)S(1)}, u32[]{:S(2)}, u32[]{:S(2)}) %collective-permute-start.4) | collective-permute-done | bytes 331808 | tf_op jit(solution)/shard_map/ppermute | solution.py:114
  38.6 3.5 %collective-permute-start.5 = (f32[9,72,128]{2,1,0:T(8,128)S(1)}, f32[9,72,128]{2,1,0:T(8,128)S(1)}, u32[]{:S(2)}, u32[]{:S(2)}) collective-permute-start(f32[9,72,128]{2,1,0:T(8,128)S(1)} %collective-permute-done.4), channel_id=1, source_target_pairs={{2,3},{6,7},{10,11},{14,15},{18,19},{22,23},{26,27},{30,31},{34,35... | collective-permute-start | bytes 995336 | tf_op jit(solution)/shard_map/ppermute | solution.py:114
  42.8 4.0 %collective-permute-done.5 = f32[9,72,128]{2,1,0:T(8,128)S(1)} collective-permute-done((f32[9,72,128]{2,1,0:T(8,128)S(1)}, f32[9,72,128]{2,1,0:T(8,128)S(1)}, u32[]{:S(2)}, u32[]{:S(2)}) %collective-permute-start.5) | collective-permute-done | bytes 331808 | tf_op jit(solution)/shard_map/ppermute | solution.py:114
  48.5 1.3 select_select_fusion.3
  50.7 3.5 %collective-permute-start.6 = (f32[36,72,128]{2,1,0:T(8,128)S(1)}, f32[36,72,128]{2,1,0:T(8,128)S(1)}, u32[]{:S(2)}, u32[]{:S(2)}) collective-permute-start(f32[36,72,128]{2,1,0:T(8,128)S(1)} %pad_maximum_fusion.1), channel_id=1, source_target_pairs={{0,4},{4,0},{8,12},{12,8},{16,20},{20,16},{24,28},{28,24},{32,36},... | collective-permute-start | bytes 3981320 | tf_op jit(solution)/shard_map/ppermute | solution.py:174
  55.5 1.5 collective-permute-done.6
  56.9 1.2 broadcast_select_fusion
  59.2 1.4 fusion.44
  60.7 1.2 gather_fusion.2
  66.0 4.6 %fusion.2 = f32[18,4,128,192]{2,3,0,1:T(8,128)S(1)} fusion(f32[18,128,128]{2,1,0:T(8,128)S(1)} %broadcast_select_fusion.1, f32[4]{0:T(128)S(1)} %multiply_add_fusion.3, s32[18]{0:T(128)S(1)} %get-tuple-element.64), kind=kOutput, calls=%fused_computation.5 | convolution fusion | flops 2721153024 | bytes 8257624 | tf_op jit(solution)/shard_map/bri,cbij->bcrj/dot_general | solution.py:138
  70.6 3.5 %fusion.23 = f32[4,192,128]{2,1,0:T(8,128)S(1)} fusion(f32[18,4,128,192]{2,3,0,1:T(8,128)S(1)} %fusion.2, s32[18]{0:T(128)S(1)} %get-tuple-element.63, s32[128]{0:T(128)S(1)} %copy-done.8), kind=kOutput, calls=%fused_computation.24 | convolution fusion | flops 2718498816 | bytes 7471688 | tf_op jit(solution)/shard_map/bcrj,bjk->crk/dot_general | solution.py:142
  74.1 23.4 %reduce-scatter.2.cloned.1.call-done = f32[4,192,128]{2,1,0:T(8,128)} async-done(((f32[4,192,512]{2,1,0:T(8,128)}), f32[4,192,128]{2,1,0:T(8,128)}) %reduce-scatter.2.cloned.1.call-update) | async-done | bytes 393232 | tf_op jit(solution)/shard_map/reduce_scatter | solution.py:171
  98.7 1.4 copy.19
  100.1 10.5 %all-to-all-start = ((f32[2,4,192,128]{3,1,0,2:T(4,128)}), f32[2,4,192,128]{3,1,0,2:T(4,128)S(1)}, u32[]{:S(2)}, u32[]{:S(2)}) async-start(f32[2,4,192,128]{3,1,0,2:T(4,128)} %copy.19), calls=%async_computation.1 | async-start | bytes 1572864 | tf_op jit(solution)/shard_map/all_to_all | solution.py:202
  110.7 27.7 %all-to-all-done = f32[2,4,192,128]{3,1,0,2:T(4,128)S(1)} async-done(((f32[2,4,192,128]{3,1,0,2:T(4,128)}), f32[2,4,192,128]{3,1,0,2:T(4,128)S(1)}, u32[]{:S(2)}, u32[]{:S(2)}) %all-to-all-start) | async-done | bytes 786464 | tf_op jit(solution)/shard_map/all_to_all | solution.py:202
  (77 shorter events, 16.1 us)
Async XLA Ops:
  6.5 91.0 %reduce-scatter.2.cloned.1.call-start = ((), (), s32[]{:S(2)}) async-start(), calls=%async_computation.2 | async-start | bytes 1966080 | tf_op jit(solution)/shard_map/reduce_scatter | solution.py:171
  9.4 1.9 %copy-start.3 = (f32[4,9,128,128]{3,2,1,0:T(8,128)S(1)}, f32[4,9,128,128]{3,2,1,0:T(8,128)}, u32[]{:S(2)}) copy-start(f32[4,9,128,128]{3,2,1,0:T(8,128)} %param.13) | copy-start | bytes 7077892
  18.3 10.6 %collective-permute-start.3 = (f32[9,72,128]{2,1,0:T(8,128)S(1)}, f32[9,72,128]{2,1,0:T(8,128)S(1)}, u32[]{:S(2)}, u32[]{:S(2)}) collective-permute-start(f32[9,72,128]{2,1,0:T(8,128)S(1)} %pad_maximum_fusion.3), channel_id=1, source_target_pairs={{0,1},{1,2},{2,3},{4,5},{5,6},{6,7},{8,9},{9,10},{10,11},{12,13},{... | collective-permute-start | bytes 995336 | tf_op jit(solution)/shard_map/ppermute | solution.py:114
  21.8 10.6 %collective-permute-start = (f32[9,72,128]{2,1,0:T(8,128)S(1)}, f32[9,72,128]{2,1,0:T(8,128)S(1)}, u32[]{:S(2)}, u32[]{:S(2)}) collective-permute-start(f32[9,72,128]{2,1,0:T(8,128)S(1)} %pad_maximum_fusion.3), channel_id=1, source_target_pairs={{1,0},{2,1},{3,2},{5,4},{6,5},{7,6},{9,8},{10,9},{11,10},{13,12},{... | collective-permute-start | bytes 995336 | tf_op jit(solution)/shard_map/ppermute | solution.py:117
  28.8 9.7 %collective-permute-start.4 = (f32[9,72,128]{2,1,0:T(8,128)S(1)}, f32[9,72,128]{2,1,0:T(8,128)S(1)}, u32[]{:S(2)}, u32[]{:S(2)}) collective-permute-start(f32[9,72,128]{2,1,0:T(8,128)S(1)} %collective-permute-done.3), channel_id=1, source_target_pairs={{1,2},{2,3},{5,6},{6,7},{9,10},{10,11},{13,14},{14,15},{17,18},{18... | collective-permute-start | bytes 995336 | tf_op jit(solution)/shard_map/ppermute | solution.py:114
  32.4 9.7 %collective-permute-start.1 = (f32[9,72,128]{2,1,0:T(8,128)S(1)}, f32[9,72,128]{2,1,0:T(8,128)S(1)}, u32[]{:S(2)}, u32[]{:S(2)}) collective-permute-start(f32[9,72,128]{2,1,0:T(8,128)S(1)} %collective-permute-done), channel_id=1, source_target_pairs={{1,0},{2,1},{5,4},{6,5},{9,8},{10,9},{13,12},{14,13},{17,16},{18,1... | collective-permute-start | bytes 995336 | tf_op jit(solution)/shard_map/ppermute | solution.py:117
  38.6 8.2 %collective-permute-start.5 = (f32[9,72,128]{2,1,0:T(8,128)S(1)}, f32[9,72,128]{2,1,0:T(8,128)S(1)}, u32[]{:S(2)}, u32[]{:S(2)}) collective-permute-start(f32[9,72,128]{2,1,0:T(8,128)S(1)} %collective-permute-done.4), channel_id=1, source_target_pairs={{2,3},{6,7},{10,11},{14,15},{18,19},{22,23},{26,27},{30,31},{34,35... | collective-permute-start | bytes 995336 | tf_op jit(solution)/shard_map/ppermute | solution.py:114
  42.1 4.7 %collective-permute-start.2 = (f32[9,72,128]{2,1,0:T(8,128)S(1)}, f32[9,72,128]{2,1,0:T(8,128)S(1)}, u32[]{:S(2)}, u32[]{:S(2)}) collective-permute-start(f32[9,72,128]{2,1,0:T(8,128)S(1)} %collective-permute-done.1), channel_id=1, source_target_pairs={{1,0},{5,4},{9,8},{13,12},{17,16},{21,20},{25,24},{29,28},{33,32},... | collective-permute-start | bytes 995336 | tf_op jit(solution)/shard_map/ppermute | solution.py:117
  46.8 0.8 copy-start.4
  47.5 0.7 copy-start.5
  49.8 0.8 copy-start.1
  49.8 0.8 copy-start.2
  50.7 4.1 %copy-start.10 = (s32[256]{0:T(256)S(1)}, s32[256]{0:T(256)}, u32[]{:S(2)}) copy-start(s32[256]{0:T(256)} %param.17) | copy-start | bytes 3076
  50.7 4.7 %copy-start.9 = (s32[4,18]{1,0:T(4,128)S(1)}, s32[4,18]{1,0:T(4,128)}, u32[]{:S(2)}) copy-start(s32[4,18]{1,0:T(4,128)} %constant.161.clone) | copy-start | bytes 868
  50.7 6.2 %collective-permute-start.6 = (f32[36,72,128]{2,1,0:T(8,128)S(1)}, f32[36,72,128]{2,1,0:T(8,128)S(1)}, u32[]{:S(2)}, u32[]{:S(2)}) collective-permute-start(f32[36,72,128]{2,1,0:T(8,128)S(1)} %pad_maximum_fusion.1), channel_id=1, source_target_pairs={{0,4},{4,0},{8,12},{12,8},{16,20},{20,16},{24,28},{28,24},{32,36},... | collective-permute-start | bytes 3981320 | tf_op jit(solution)/shard_map/ppermute | solution.py:174
  58.2 1.1 copy-start
  63.1 1.3 slice-start
  66.0 4.6 %copy-start.8 = (s32[128]{0:T(128)S(1)}, s32[128]{0:T(128)}, u32[]{:S(2)}) copy-start(s32[128]{0:T(128)} %iota_add_fusion) | copy-start | bytes 1540
  70.5 27.0 %copy-start.6 = (s32[4,192,128]{2,1,0:T(8,128)S(1)}, s32[4,192,128]{2,1,0:T(8,128)}, u32[]{:S(2)}) copy-start(s32[4,192,128]{2,1,0:T(8,128)} %param.16) | copy-start | bytes 1179652
  70.6 27.0 %copy-start.7 = (f32[4]{0:T(128)S(1)}, f32[4]{0:T(128)}, u32[]{:S(2)}) copy-start(f32[4]{0:T(128)} %dynamic-slice_convert_fusion) | copy-start | bytes 52
  100.1 38.3 %all-to-all-start = ((f32[2,4,192,128]{3,1,0,2:T(4,128)}), f32[2,4,192,128]{3,1,0,2:T(4,128)S(1)}, u32[]{:S(2)}, u32[]{:S(2)}) async-start(f32[2,4,192,128]{3,1,0,2:T(4,128)} %copy.19), calls=%async_computation.1 | async-start | bytes 1572864 | tf_op jit(solution)/shard_map/all_to_all | solution.py:202
Sparse Core Ops, SparseCore 0:
  54.4 43.0 reduce-scatter.1

commit v10 on v7

--- a/solution.py
+++ b/solution.py
@@ -99,13 +99,13 @@
         == lax.broadcasted_iota(jnp.int32, (1, side, MOS_COLS), 1) + col_start[:, None, None]
     ).astype(jnp.float32)
     rows_placed = jnp.einsum(
-        "bri,acbij->bacrj", row_hit, stacked, precision=lax.Precision.HIGHEST,
+        "bri,acbij->bacrj", row_hit, stacked, precision=lax.Precision.HIGH,
         preferred_element_type=jnp.float32,
     )
     blocks = lax.psum(1, "beam")
     col_hit = col_hit.reshape(col_hit.shape[0], side, blocks, MOS_COLS // blocks)
     planes = jnp.einsum(
-        "bacrj,bjnk->nacrk", rows_placed, col_hit, precision=lax.Precision.HIGHEST,
+        "bacrj,bjnk->nacrk", rows_placed, col_hit, precision=lax.Precision.HIGH,
         preferred_element_type=jnp.float32,
     )
     own = lax.psum_scatter(planes, "beam", scatter_dimension=0, tiled=False)

time: 140 us -> 137 us (0.979)
  matrix products: 12.8 us -> 9.54 us
    dot_general x1, matrix products: 8.13 us -> 6.08 us  [local(): jnp.einsum('bacrj,bjnk->nacrk', rows_placed, col_hit, precision=lax.Preci...]
where the time goes in v10:
time: 137 us; the launch traced here: 136 us
  waiting for transfers between devices  94.8 us (69%)
  between operations  13.5 us (10%)
  starting transfers between devices  10.5 us (8%)
  matrix products  9.54 us (7%)
  local copies, waits for them, and re-layouts  5.42 us (4%)
  other arithmetic  2.53 us (2%)
    reduce_scatter x1, waiting for transfers between devices, local(): own = lax.psum_scatter(planes, 'beam', scatter_dimension=0, tiled=False)  67.1 us
    all_to_all x1, waiting for transfers between devices, local(): lax.all_to_all(jnp.stack([celestial_image, importance_factor]), 'chan', s...  27.7 us
    all_to_all x1, starting transfers between devices, local(): lax.all_to_all(jnp.stack([celestial_image, importance_factor]), 'chan', s...  10.5 us
    dot_general x1, matrix products, local(): jnp.einsum('bacrj,bjnk->nacrk', rows_placed, col_hit, precision=lax.Preci...  6.08 us
  transfers between devices with their start and end apart: 2, of which 2 were waited for; matrix products, arithmetic and copies ran while one was open for 0% of the time, Pallas kernels for 0%

profile of v10, /device:TPU:65, one launch (start us, length us, event | category | flops | bytes accessed | tf_op | source)
XLA Modules:
  0.0 136.3 jit_solution(8376947917615958476)
XLA Ops:
  6.6 1.3 log.3
  7.9 0.4 exponential_multiply_fusion
  8.2 0.1 copy-done
  8.4 0.4 multiply_bitcast_fusion
  8.8 0.3 copy-done.2
  9.1 2.2 %fusion.2 = f32[9,2,4,128,192]{3,4,0,2,1:T(8,128)S(1)} fusion(f32[1,4,9,128,128]{4,3,2,1,0:T(8,128)S(1)} %exponential_multiply_fusion, f32[1,4,9,128,128]{4,3,2,1,0:T(8,128)S(1)} %multiply_bitcast_fusion, s32[9]{0:T(128)S(1)} %get-tuple-element.23), kind=kOutput, calls=%fused_computation.2 | convolution fusion | flops 1360576512 | bytes 11796516 | tf_op jit(solution)/shard_map/bri,acbij->bacrj/dot_general | solution.py:101
  11.3 6.1 %fusion.8 = f32[4,2,4,192,128]{4,3,2,1,0:T(8,128)} fusion(f32[9,2,4,128,192]{3,4,0,2,1:T(8,128)S(1)} %fusion.2, s32[9]{0:T(128)S(1)} %get-tuple-element.22, s32[4,128]{1,0:T(4,128)S(1)} %multiply_add_fusion.1), kind=kOutput, calls=%fused_computation.10 | convolution fusion | flops 5436997632 | bytes 10225700 | tf_op jit(solution)/shard_map/bacrj,bjnk->nacrk/dot_general | solution.py:107
  17.4 0.7 copy-done.3
  18.1 67.1 %reduce-scatter.2.cloned.1.call-done = f32[1,2,4,192,128]{4,3,2,1,0:T(8,128)} async-done(((f32[4,2,4,192,128]{4,3,2,1,0:T(8,128)}), f32[1,2,4,192,128]{4,3,2,1,0:T(8,128)}) %reduce-scatter.2.cloned.1.call-update) | async-done | bytes 786448 | tf_op jit(solution)/shard_map/reduce_scatter | solution.py:111
  85.2 1.2 fusion.24
  86.5 1.4 %copy.14 = f32[2,4,192,128]{3,1,0,2:T(4,128)} copy(f32[2,4,192,128]{3,2,1,0:T(8,128)S(1)} %pad_maximum_fusion) | data formatting | bytes 1572864 | tf_op jit(solution)/shard_map/stack | solution.py:123
  87.9 10.5 %all-to-all-start = ((f32[2,4,192,128]{3,1,0,2:T(4,128)}), f32[2,4,192,128]{3,1,0,2:T(4,128)S(1)}, u32[]{:S(2)}, u32[]{:S(2)}) async-start(f32[2,4,192,128]{3,1,0,2:T(4,128)} %copy.14), calls=%async_computation.1 | async-start | bytes 1572864 | tf_op jit(solution)/shard_map/all_to_all | solution.py:122
  98.6 27.7 %all-to-all-done = f32[2,4,192,128]{3,1,0,2:T(4,128)S(1)} async-done(((f32[2,4,192,128]{3,1,0,2:T(4,128)}), f32[2,4,192,128]{3,1,0,2:T(4,128)S(1)}, u32[]{:S(2)}, u32[]{:S(2)}) %all-to-all-start) | async-done | bytes 786464 | tf_op jit(solution)/shard_map/all_to_all | solution.py:122
  126.3 0.1 copy.15
  126.4 0.1 fusion.61
  126.5 0.1 copy.16
  126.6 0.1 copy.17
  126.8 0.3 fusion.18
  127.1 0.3 fusion.20
  127.4 0.1 fusion.44
  127.6 0.7 convolution_subtract_fusion
  128.2 0.1 multiply_add_fusion
  128.3 0.2 copy.18
  128.5 0.9 copy.19
  (24 shorter events, 0.4 us)
Async XLA Ops:
  6.5 1.8 %copy-start = (f32[4,9,128,128]{3,2,1,0:T(8,128)S(1)}, f32[4,9,128,128]{3,2,1,0:T(8,128)}, u32[]{:S(2)}) copy-start(f32[4,9,128,128]{3,2,1,0:T(8,128)} %param.5) | copy-start | bytes 7077892
  6.5 78.7 %reduce-scatter.2.cloned.1.call-start = ((), (), s32[]{:S(2)}) async-start(), calls=%async_computation.2 | async-start | bytes 3932160 | tf_op jit(solution)/shard_map/reduce_scatter | solution.py:111
  8.4 0.7 copy-start.2
  17.4 0.7 copy-start.3
  17.4 67.8 %copy-start.1 = (s32[4,192,128]{2,1,0:T(8,128)S(1)}, s32[4,192,128]{2,1,0:T(8,128)}, u32[]{:S(2)}) copy-start(s32[4,192,128]{2,1,0:T(8,128)} %param.8) | copy-start | bytes 1179652
  87.9 38.3 %all-to-all-start = ((f32[2,4,192,128]{3,1,0,2:T(4,128)}), f32[2,4,192,128]{3,1,0,2:T(4,128)S(1)}, u32[]{:S(2)}, u32[]{:S(2)}) async-start(f32[2,4,192,128]{3,1,0,2:T(4,128)} %copy.14), calls=%async_computation.1 | async-start | bytes 1572864 | tf_op jit(solution)/shard_map/all_to_all | solution.py:122
Sparse Core Ops, SparseCore 0:
  17.5 67.6 reduce-scatter.1

commit v11 on v10

--- a/solution.py
+++ b/solution.py
@@ -78,6 +78,19 @@
     return smoothed.reshape(channels, rows, columns)
 
 
+def exact_onehot_dot(spec, first, second, data_first):
+    data = first if data_first else second
+    wide = lax.reduce_precision(data, exponent_bits=8, mantissa_bits=15)
+    rest = data - wide
+    parts = []
+    for piece, precision in ((wide, lax.Precision.HIGH), (rest, lax.Precision.DEFAULT)):
+        operands = (piece, second) if data_first else (first, piece)
+        parts.append(
+            jnp.einsum(spec, *operands, precision=precision, preferred_element_type=jnp.float32)
+        )
+    return parts[0] + parts[1]
+
+
 def local(images, beam_weight, offsets, rejected_indicator, regression_indicator):
     ch_dev = images.shape[0]
     side = images.shape[2]
@@ -98,16 +111,10 @@
         lax.broadcasted_iota(jnp.int32, (1, side, MOS_COLS), 2)
         == lax.broadcasted_iota(jnp.int32, (1, side, MOS_COLS), 1) + col_start[:, None, None]
     ).astype(jnp.float32)
-    rows_placed = jnp.einsum(
-        "bri,acbij->bacrj", row_hit, stacked, precision=lax.Precision.HIGH,
-        preferred_element_type=jnp.float32,
-    )
+    rows_placed = exact_onehot_dot("bri,acbij->bacrj", row_hit, stacked, data_first=False)
     blocks = lax.psum(1, "beam")
     col_hit = col_hit.reshape(col_hit.shape[0], side, blocks, MOS_COLS // blocks)
-    planes = jnp.einsum(
-        "bacrj,bjnk->nacrk", rows_placed, col_hit, precision=lax.Precision.HIGH,
-        preferred_element_type=jnp.float32,
-    )
+    planes = exact_onehot_dot("bacrj,bjnk->nacrk", rows_placed, col_hit, data_first=True)
     own = lax.psum_scatter(planes, "beam", scatter_dimension=0, tiled=False)
     dividend_accumulator = own[0]
     normalizer_accumulated = own[1]

time: 137 us -> 145 us (1.058)
  matrix products: 9.54 us -> 17.9 us
    dot_general x2 -> x4, matrix products: 8.31 us -> 16.7 us  [exact_onehot_dot(): jnp.einsum(spec, *operands, precision=precision, preferred_element_type=j...]
where the time goes in v11:
time: 145 us
  waiting for transfers between devices  94.8 us (65%)
  matrix products  17.9 us (12%)
  between operations  13.5 us (9%)
  starting transfers between devices  10.5 us (7%)
  local copies, waits for them, and re-layouts  5.36 us (4%)
  other arithmetic  2.6 us (2%)
    reduce_scatter x1, waiting for transfers between devices, local(): own = lax.psum_scatter(planes, 'beam', scatter_dimension=0, tiled=False)  67.1 us
    all_to_all x1, waiting for transfers between devices, local(): lax.all_to_all(jnp.stack([celestial_image, importance_factor]), 'chan', s...  27.7 us
    dot_general x4, matrix products, exact_onehot_dot(): jnp.einsum(spec, *operands, precision=precision, preferred_element_type=j...  16.7 us
    all_to_all x1, starting transfers between devices, local(): lax.all_to_all(jnp.stack([celestial_image, importance_factor]), 'chan', s...  10.5 us
  transfers between devices with their start and end apart: 2, of which 2 were waited for; matrix products, arithmetic and copies ran while one was open for 0% of the time, Pallas kernels for 0%

profile of v11, /device:TPU:65, one launch (start us, length us, event | category | flops | bytes accessed | tf_op | source)
XLA Modules:
  0.0 144.7 jit_solution(1709666908221651320)
XLA Ops:
  6.6 1.3 log.3
  7.9 0.4 exponential_multiply_fusion
  8.2 0.1 copy-done
  8.4 0.4 fusion.10
  8.8 0.2 copy-done.2
  9.1 1.7 %fusion.8 = f32[9,2,4,128,192]{3,4,2,1,0:T(8,128)S(1)} fusion(f32[1,4,9,128,128]{4,3,1,0,2:T(8,128)S(1)} %exponential_multiply_fusion, f32[1,4,9,128,128]{4,3,1,0,2:T(8,128)S(1)} %fusion.10, s32[9]{0:T(128)S(1)} %get-tuple-element.23), kind=kOutput, calls=%fused_computation.11 | convolution fusion | flops 456966144 | bytes 11796516 | tf_op jit(solution)/shard_map/bri,acbij->bacrj/dot_general | solution.py:89
  10.8 5.3 %bitcast_subtract_fusion = (bf16[9,2,4,192,128]{4,3,2,1,0:T(8,128)(2,1)S(1)}, f32[9,2,4,128,192]{3,4,2,1,0:T(8,128)S(1)}) fusion(f32[9,2,4,128,192]{3,4,2,1,0:T(8,128)S(1)} %fusion.8, s32[9]{0:T(128)S(1)} %get-tuple-element.23, f32[1,4,9,128,128]{4,3,1,0,2:T(8,128)S(1)} %exponential_multiply_fusion, f32[1,4,9,128,128]{4,3,1,0,2:T(8,128)S(1)} %fusion.10), kind=kOutput, calls=%fused_computation.4 | convolution fusion | flops 1368834048 | bytes 22413348 | tf_op jit(solution)/shard_map/bri,acbij->bacrj/dot_general | solution.py:89
  16.1 2.3 %fusion = f32[4,128,2,4,192,1]{1,4,5,3,2,0:T(8,128)S(1)} fusion(bf16[9,2,4,192,128]{4,3,2,1,0:T(8,128)(2,1)S(1)} %get-tuple-element.24, s32[9]{0:T(128)S(1)} %get-tuple-element.22, s32[4,128]{1,0:T(4,128)S(1)} %multiply_add_fusion.1), kind=kOutput, calls=%fused_computation | convolution fusion | flops 1813118976 | bytes 6686756 | tf_op jit(solution)/shard_map/bacrj,bjnk->nacrk/dot_general | solution.py:89
  18.5 7.3 %fusion.9 = f32[4,2,4,192,128]{4,3,2,1,0:T(8,128)} fusion(f32[4,128,2,4,192,1]{1,4,5,3,2,0:T(8,128)S(1)} %fusion, s32[9]{0:T(128)S(1)} %get-tuple-element.22, s32[4,128]{1,0:T(4,128)S(1)} %multiply_add_fusion.1, f32[9,2,4,128,192]{3,4,2,1,0:T(8,128)S(1)} %get-tuple-element.25, f32[9,2,4,128,192]{3,4,2,1,0:T(8,128)S(1)} %fusion.8), kind=kOutput, calls=%fused_computation.14 | convolution fusion | flops 5441323008 | bytes 20449316 | tf_op jit(solution)/shard_map/bacrj,bjnk->nacrk/dot_general | solution.py:89
  25.8 0.7 copy-done.3
  26.5 67.1 %reduce-scatter.2.cloned.1.call-done = f32[1,2,4,192,128]{4,3,2,1,0:T(8,128)} async-done(((f32[4,2,4,192,128]{4,3,2,1,0:T(8,128)}), f32[1,2,4,192,128]{4,3,2,1,0:T(8,128)}) %reduce-scatter.2.cloned.1.call-update) | async-done | bytes 786448 | tf_op jit(solution)/shard_map/reduce_scatter | solution.py:118
  93.6 1.2 fusion.31
  94.9 1.4 copy.23
  96.3 10.5 %all-to-all-start = ((f32[2,4,192,128]{3,1,0,2:T(4,128)}), f32[2,4,192,128]{3,1,0,2:T(4,128)S(1)}, u32[]{:S(2)}, u32[]{:S(2)}) async-start(f32[2,4,192,128]{3,1,0,2:T(4,128)} %copy.23), calls=%async_computation.1 | async-start | bytes 1572864 | tf_op jit(solution)/shard_map/all_to_all | solution.py:129
  106.9 27.7 %all-to-all-done = f32[2,4,192,128]{3,1,0,2:T(4,128)S(1)} async-done(((f32[2,4,192,128]{3,1,0,2:T(4,128)}), f32[2,4,192,128]{3,1,0,2:T(4,128)S(1)}, u32[]{:S(2)}, u32[]{:S(2)}) %all-to-all-start) | async-done | bytes 786464 | tf_op jit(solution)/shard_map/all_to_all | solution.py:129
  134.6 0.1 copy.24
  134.9 0.1 copy.25
  135.0 0.1 copy.26
  135.1 0.3 fusion.25
  135.4 0.3 fusion.27
  135.9 0.7 convolution_subtract_fusion
  136.6 0.1 multiply_add_fusion
  136.7 0.2 copy.27
  136.9 0.9 copy.28
  (26 shorter events, 0.6 us)
Async XLA Ops:
  6.5 1.8 %copy-start = (f32[4,9,128,128]{3,2,1,0:T(8,128)S(1)}, f32[4,9,128,128]{3,2,1,0:T(8,128)}, u32[]{:S(2)}) copy-start(f32[4,9,128,128]{3,2,1,0:T(8,128)} %param.5) | copy-start | bytes 7077892
  6.5 87.1 %reduce-scatter.2.cloned.1.call-start = ((), (), s32[]{:S(2)}) async-start(), calls=%async_computation.2 | async-start | bytes 3932160 | tf_op jit(solution)/shard_map/reduce_scatter | solution.py:118
  8.4 0.7 copy-start.2
  25.8 0.7 copy-start.3
  25.8 67.8 %copy-start.1 = (s32[4,192,128]{2,1,0:T(8,128)S(1)}, s32[4,192,128]{2,1,0:T(8,128)}, u32[]{:S(2)}) copy-start(s32[4,192,128]{2,1,0:T(8,128)} %param.8) | copy-start | bytes 1179652
  96.3 38.3 %all-to-all-start = ((f32[2,4,192,128]{3,1,0,2:T(4,128)}), f32[2,4,192,128]{3,1,0,2:T(4,128)S(1)}, u32[]{:S(2)}, u32[]{:S(2)}) async-start(f32[2,4,192,128]{3,1,0,2:T(4,128)} %copy.23), calls=%async_computation.1 | async-start | bytes 1572864 | tf_op jit(solution)/shard_map/all_to_all | solution.py:129
Sparse Core Ops, SparseCore 0:
  25.9 67.6 reduce-scatter.1

commit v12 on v7

--- a/solution.py
+++ b/solution.py
@@ -119,10 +119,15 @@
     importance_factor = normalizer_accumulated * (
         emission_absent[:, None, None] * accepted_entries + 0.01
     )
-    arrived = lax.all_to_all(
-        jnp.stack([celestial_image, importance_factor]), "chan", split_axis=2, concat_axis=1, tiled=True
-    )
-    return clean_pair((arrived[0], arrived[1]))
+    both = jnp.stack([celestial_image, importance_factor])
+    kinds, chans, rows, cols = both.shape
+    both = both.transpose(2, 0, 1, 3).reshape(rows, kinds * chans, cols)
+    both = lax.all_to_all(both, "chan", split_axis=0, concat_axis=0, tiled=True)
+    sources = all_channels // chans
+    rows_dev = rows // sources
+    both = both.reshape(sources, rows_dev, kinds, chans, cols).transpose(2, 0, 3, 1, 4)
+    both = both.reshape(kinds, all_channels, rows_dev, cols)
+    return clean_pair((both[0], both[1]))
 
 
 def solution(mesh):

time: 140 us -> 140 us (level)
    another operation x1 -> x0, local copies, waits for them, and re-layouts: 1.41 us -> none  [local(): jnp.stack([celestial_image, importance_factor])]
where the time goes in v12:
time: 140 us; the launch traced here: 139 us
  waiting for transfers between devices  94.8 us (68%)
  between operations  13.5 us (10%)
  matrix products  12.8 us (9%)
  starting transfers between devices  10.5 us (8%)
  local copies, waits for them, and re-layouts  5.29 us (4%)
  other arithmetic  2.53 us (2%)
    reduce_scatter x1, waiting for transfers between devices, local(): own = lax.psum_scatter(planes, 'beam', scatter_dimension=0, tiled=False)  67.1 us
    all_to_all x1, waiting for transfers between devices, local(): both = lax.all_to_all(both, 'chan', split_axis=0, concat_axis=0, tiled=True)  27.7 us
    all_to_all x1, starting transfers between devices, local(): both = lax.all_to_all(both, 'chan', split_axis=0, concat_axis=0, tiled=True)  10.5 us
    dot_general x1, matrix products, local(): jnp.einsum('bacrj,bjnk->nacrk', rows_placed, col_hit, precision=lax.Preci...  8.13 us
    dot_general x1, matrix products, local(): jnp.einsum('bri,acbij->bacrj', row_hit, stacked, precision=lax.Precision....  3.43 us
  transfers between devices with their start and end apart: 2, of which 2 were waited for; matrix products, arithmetic and copies ran while one was open for 0% of the time, Pallas kernels for 0%

profile of v12, /device:TPU:65, one launch (start us, length us, event | category | flops | bytes accessed | tf_op | source)
XLA Modules:
  0.0 139.4 jit_solution(4114490680864622450)
XLA Ops:
  6.6 1.3 log.3
  7.9 0.4 exponential_multiply_fusion
  8.2 0.1 copy-done
  8.4 0.4 multiply_bitcast_fusion
  8.8 0.3 copy-done.2
  9.1 3.4 %fusion.2 = f32[9,2,4,128,192]{3,4,0,2,1:T(8,128)S(1)} fusion(f32[1,4,9,128,128]{4,3,2,1,0:T(8,128)S(1)} %exponential_multiply_fusion, f32[1,4,9,128,128]{4,3,2,1,0:T(8,128)S(1)} %multiply_bitcast_fusion, s32[9]{0:T(128)S(1)} %get-tuple-element.23), kind=kOutput, calls=%fused_computation.2 | convolution fusion | flops 2719531008 | bytes 11796516 | tf_op jit(solution)/shard_map/bri,acbij->bacrj/dot_general | solution.py:101
  12.5 8.1 %fusion.8 = f32[4,2,4,192,128]{4,3,2,1,0:T(8,128)} fusion(f32[9,2,4,128,192]{3,4,0,2,1:T(8,128)S(1)} %fusion.2, s32[9]{0:T(128)S(1)} %get-tuple-element.22, s32[4,128]{1,0:T(4,128)S(1)} %multiply_add_fusion.1), kind=kOutput, calls=%fused_computation.10 | convolution fusion | flops 10872815616 | bytes 10225700 | tf_op jit(solution)/shard_map/bacrj,bjnk->nacrk/dot_general | solution.py:107
  20.7 0.7 copy-done.3
  21.3 0.1 dynamic-slice_convert_fusion
  21.4 67.1 %reduce-scatter.2.cloned.1.call-done = f32[1,2,4,192,128]{4,3,2,1,0:T(8,128)} async-done(((f32[4,2,4,192,128]{4,3,2,1,0:T(8,128)}), f32[1,2,4,192,128]{4,3,2,1,0:T(8,128)}) %reduce-scatter.2.cloned.1.call-update) | async-done | bytes 786448 | tf_op jit(solution)/shard_map/reduce_scatter | solution.py:111
  88.5 1.2 fusion.24
  89.8 1.4 copy.13
  91.1 10.5 %all-to-all-start = ((f32[192,8,128]{2,1,0:T(8,128)}), f32[192,8,128]{2,1,0:T(8,128)S(1)}, u32[]{:S(2)}, u32[]{:S(2)}) async-start(f32[192,8,128]{2,1,0:T(8,128)} %copy.13), calls=%async_computation.1 | async-start | bytes 1572864 | tf_op jit(solution)/shard_map/all_to_all | solution.py:125
  101.8 27.7 %all-to-all-done = f32[192,8,128]{2,1,0:T(8,128)S(1)} async-done(((f32[192,8,128]{2,1,0:T(8,128)}), f32[192,8,128]{2,1,0:T(8,128)S(1)}, u32[]{:S(2)}, u32[]{:S(2)}) %all-to-all-start) | async-done | bytes 786464 | tf_op jit(solution)/shard_map/all_to_all | solution.py:125
  129.5 0.1 fusion.61
  129.6 0.1 copy.14
  129.7 0.1 copy.15
  129.9 0.3 fusion.18
  130.2 0.3 fusion.20
  130.5 0.1 fusion.44
  130.7 0.7 convolution_subtract_fusion
  131.3 0.1 multiply_add_fusion
  131.5 0.2 copy.16
  131.6 0.9 copy.17
  (23 shorter events, 0.4 us)
Async XLA Ops:
  6.5 1.8 %copy-start = (f32[4,9,128,128]{3,2,1,0:T(8,128)S(1)}, f32[4,9,128,128]{3,2,1,0:T(8,128)}, u32[]{:S(2)}) copy-start(f32[4,9,128,128]{3,2,1,0:T(8,128)} %param.5) | copy-start | bytes 7077892
  6.5 81.9 %reduce-scatter.2.cloned.1.call-start = ((), (), s32[]{:S(2)}) async-start(), calls=%async_computation.2 | async-start | bytes 3932160 | tf_op jit(solution)/shard_map/reduce_scatter | solution.py:111
  8.4 0.7 copy-start.2
  20.6 0.7 copy-start.3
  20.6 67.8 %copy-start.1 = (s32[4,192,128]{2,1,0:T(8,128)S(1)}, s32[4,192,128]{2,1,0:T(8,128)}, u32[]{:S(2)}) copy-start(s32[4,192,128]{2,1,0:T(8,128)} %param.8) | copy-start | bytes 1179652
  91.1 38.3 %all-to-all-start = ((f32[192,8,128]{2,1,0:T(8,128)}), f32[192,8,128]{2,1,0:T(8,128)S(1)}, u32[]{:S(2)}, u32[]{:S(2)}) async-start(f32[192,8,128]{2,1,0:T(8,128)} %copy.13), calls=%async_computation.1 | async-start | bytes 1572864 | tf_op jit(solution)/shard_map/all_to_all | solution.py:125
Sparse Core Ops, SparseCore 0:
  20.8 67.6 reduce-scatter.1

commit v13 on v11

--- a/solution.py
+++ b/solution.py
@@ -114,7 +114,10 @@
     rows_placed = exact_onehot_dot("bri,acbij->bacrj", row_hit, stacked, data_first=False)
     blocks = lax.psum(1, "beam")
     col_hit = col_hit.reshape(col_hit.shape[0], side, blocks, MOS_COLS // blocks)
-    planes = exact_onehot_dot("bacrj,bjnk->nacrk", rows_placed, col_hit, data_first=True)
+    planes = jnp.einsum(
+        "bacrj,bjnk->nacrk", rows_placed, col_hit, precision=lax.Precision.HIGHEST,
+        preferred_element_type=jnp.float32,
+    )
     own = lax.psum_scatter(planes, "beam", scatter_dimension=0, tiled=False)
     dividend_accumulator = own[0]
     normalizer_accumulated = own[1]

time: 145 us -> 141 us (0.972)
  matrix products: 17.9 us -> 14.1 us
    dot_general x4 -> x2, matrix products: 16.7 us -> 4.59 us  [exact_onehot_dot(): jnp.einsum(spec, *operands, precision=precision, preferred_element_type=j...]
    dot_general x0 -> x1, matrix products: none -> 8.23 us  [local(): jnp.einsum('bacrj,bjnk->nacrk', rows_placed, col_hit, precision=lax.Preci...]
where the time goes in v13:
time: 141 us
  waiting for transfers between devices  94.8 us (67%)
  matrix products  14.1 us (10%)
  between operations  13.5 us (10%)
  starting transfers between devices  10.7 us (8%)
  local copies, waits for them, and re-layouts  5.37 us (4%)
  other arithmetic  2.59 us (2%)
    reduce_scatter x1, waiting for transfers between devices, local(): own = lax.psum_scatter(planes, 'beam', scatter_dimension=0, tiled=False)  67.1 us
    all_to_all x1, waiting for transfers between devices, local(): lax.all_to_all(jnp.stack([celestial_image, importance_factor]), 'chan', s...  27.7 us
    all_to_all x1, starting transfers between devices, local(): lax.all_to_all(jnp.stack([celestial_image, importance_factor]), 'chan', s...  10.6 us
    dot_general x1, matrix products, local(): jnp.einsum('bacrj,bjnk->nacrk', rows_placed, col_hit, precision=lax.Preci...  8.23 us
    dot_general x2, matrix products, exact_onehot_dot(): jnp.einsum(spec, *operands, precision=precision, preferred_element_type=j...  4.59 us
  transfers between devices with their start and end apart: 2, of which 2 were waited for; matrix products, arithmetic and copies ran while one was open for 0% of the time, Pallas kernels for 0%

profile of v13, /device:TPU:65, one launch (start us, length us, event | category | flops | bytes accessed | tf_op | source)
XLA Modules:
  0.0 141.0 jit_solution(13161719047720778422)
XLA Ops:
  6.5 1.3 log.3
  7.8 0.4 exponential_multiply_fusion
  8.2 0.1 copy-done
  8.4 0.4 multiply_bitcast_fusion
  8.8 0.2 copy-done.2
  9.1 1.7 %fusion.5 = f32[9,2,4,128,192]{3,4,0,2,1:T(8,128)S(1)} fusion(f32[1,4,9,128,128]{4,3,2,1,0:T(8,128)S(1)} %exponential_multiply_fusion, f32[1,4,9,128,128]{4,3,2,1,0:T(8,128)S(1)} %multiply_bitcast_fusion, s32[9]{0:T(128)S(1)} %get-tuple-element.23), kind=kOutput, calls=%fused_computation.6 | convolution fusion | flops 456966144 | bytes 11796516 | tf_op jit(solution)/shard_map/bri,acbij->bacrj/dot_general | solution.py:89
  10.8 2.9 %fusion.3 = f32[9,2,4,128,192]{3,4,0,2,1:T(8,128)S(1)} fusion(f32[1,4,9,128,128]{4,3,2,1,0:T(8,128)S(1)} %exponential_multiply_fusion, f32[1,4,9,128,128]{4,3,2,1,0:T(8,128)S(1)} %multiply_bitcast_fusion, s32[9]{0:T(128)S(1)} %get-tuple-element.23), kind=kOutput, calls=%fused_computation.4 | convolution fusion | flops 1361756160 | bytes 11796516 | tf_op jit(solution)/shard_map/bri,acbij->bacrj/dot_general | solution.py:89
  13.7 8.2 %fusion.8 = f32[4,2,4,192,128]{4,3,2,1,0:T(8,128)} fusion(f32[9,2,4,128,192]{3,4,0,2,1:T(8,128)S(1)} %fusion.3, f32[9,2,4,128,192]{3,4,0,2,1:T(8,128)S(1)} %fusion.5, s32[9]{0:T(128)S(1)} %get-tuple-element.22, s32[4,128]{1,0:T(4,128)S(1)} %multiply_add_fusion.1), kind=kOutput, calls=%fused_computation.12 | convolution fusion | flops 10874585088 | bytes 17303588 | tf_op jit(solution)/shard_map/bacrj,bjnk->nacrk/dot_general | solution.py:117
  21.9 0.7 copy-done.3
  22.7 67.1 %reduce-scatter.2.cloned.1.call-done = f32[1,2,4,192,128]{4,3,2,1,0:T(8,128)} async-done(((f32[4,2,4,192,128]{4,3,2,1,0:T(8,128)}), f32[1,2,4,192,128]{4,3,2,1,0:T(8,128)}) %reduce-scatter.2.cloned.1.call-update) | async-done | bytes 786448 | tf_op jit(solution)/shard_map/reduce_scatter | solution.py:121
  89.7 1.2 fusion.26
  91.0 1.4 copy.14
  92.4 10.6 %all-to-all-start = ((f32[2,4,192,128]{3,1,0,2:T(4,128)}), f32[2,4,192,128]{3,1,0,2:T(4,128)S(1)}, u32[]{:S(2)}, u32[]{:S(2)}) async-start(f32[2,4,192,128]{3,1,0,2:T(4,128)} %copy.14), calls=%async_computation.1 | async-start | bytes 1572864 | tf_op jit(solution)/shard_map/all_to_all | solution.py:132
  103.3 27.7 %all-to-all-done = f32[2,4,192,128]{3,1,0,2:T(4,128)S(1)} async-done(((f32[2,4,192,128]{3,1,0,2:T(4,128)}), f32[2,4,192,128]{3,1,0,2:T(4,128)S(1)}, u32[]{:S(2)}, u32[]{:S(2)}) %all-to-all-start) | async-done | bytes 786464 | tf_op jit(solution)/shard_map/all_to_all | solution.py:132
  131.0 0.1 copy.15
  131.2 0.1 copy.16
  131.3 0.1 copy.17
  131.5 0.3 fusion.20
  131.8 0.3 fusion.22
  132.1 0.1 fusion.46
  132.3 0.7 convolution_subtract_fusion
  132.9 0.1 multiply_add_fusion
  133.1 0.2 copy.18
  133.2 0.9 copy.19
  (25 shorter events, 0.5 us)
Async XLA Ops:
  6.5 1.8 %copy-start = (f32[4,9,128,128]{3,2,1,0:T(8,128)S(1)}, f32[4,9,128,128]{3,2,1,0:T(8,128)}, u32[]{:S(2)}) copy-start(f32[4,9,128,128]{3,2,1,0:T(8,128)} %param.5) | copy-start | bytes 7077892
  6.5 83.2 %reduce-scatter.2.cloned.1.call-start = ((), (), s32[]{:S(2)}) async-start(), calls=%async_computation.2 | async-start | bytes 3932160 | tf_op jit(solution)/shard_map/reduce_scatter | solution.py:121
  8.4 0.7 copy-start.2
  21.9 0.7 copy-start.3
  21.9 67.8 %copy-start.1 = (s32[4,192,128]{2,1,0:T(8,128)S(1)}, s32[4,192,128]{2,1,0:T(8,128)}, u32[]{:S(2)}) copy-start(s32[4,192,128]{2,1,0:T(8,128)} %param.8) | copy-start | bytes 1179652
  92.4 38.5 %all-to-all-start = ((f32[2,4,192,128]{3,1,0,2:T(4,128)}), f32[2,4,192,128]{3,1,0,2:T(4,128)S(1)}, u32[]{:S(2)}, u32[]{:S(2)}) async-start(f32[2,4,192,128]{3,1,0,2:T(4,128)} %copy.14), calls=%async_computation.1 | async-start | bytes 1572864 | tf_op jit(solution)/shard_map/all_to_all | solution.py:132
Sparse Core Ops, SparseCore 0:
  22.1 67.6 reduce-scatter.1
